TPU v7x, 128 devices: a whole 4x4x4 slice. The times are simulated.
128 devices in a mesh: grp: 4 (over z), dev: 32 (over x, y, core).
Axes of the slice: x: 4, y: 4, z: 4, core: 2. Of those that a mesh axis runs over, the one named last changes fastest.
Arguments:
- packed_w: bfloat16 [4, 8192, 8192], P(None, 'dev', 'grp'), may hold values from -0.0625 to 0.0625
- packed_t: bfloat16 [4, 8192, 1536], P(None, 'dev', 'grp'), may hold values from -6 to 6
- row_energy: float32 [4, 8192], P('grp', 'dev'), may hold values from 0.3 to 4
- col_energy: float32 [4, 1536], P('grp'), may hold values from 0.3 to 4
- block_order: int32 [4], replicated, may hold values from 3072 to 8192, as said below
Outputs:
- new_amps: float32 [4, 8192, 1536], P(None, 'dev', 'grp')
Inputs may be any that keep to these rules, and one draw needn't show every extreme that they name: `block_order`: one block has order exactly 8192; the others lie between 3072 and 8191.
All inputs are finite; a program needn't handle non-finite values.
Results may differ from a plain program's by a relative error of at most 0.0003.
Values may be sent and summed in bfloat16 or wider, within the bound.
No kernel may reach another device: no remote copies, remote signals or barrier semaphores. Data moves between devices by JAX's collectives and lax.ppermute only.
A program may use at most 192 MiB of HBM per device.

v0:
```python
import jax
import jax.numpy as jnp
from jax import lax
from jax.sharding import PartitionSpec as P


def trimmed_product(w_rows, whole, order, ndev, local):
    columns = whole.shape[1]
    stacked = whole.reshape(ndev, local, columns)
    w_split = w_rows.reshape(local, ndev, local)
    width = min(64, local)
    depth = (order + ndev - 1) // ndev
    turns = (depth + width - 1) // width

    def step_block(turn, total):
        begin = (turn * width).astype(jnp.int32)
        part_w = lax.dynamic_slice_in_dim(w_split, begin, width, 2)
        part_t = lax.dynamic_slice_in_dim(stacked, begin, width, 1)
        return total + jnp.einsum("pnb,nbc->pc", part_w, part_t, preferred_element_type=jnp.float32)

    return lax.fori_loop(0, turns, step_block, jnp.zeros((local, columns), jnp.float32))


def apply_update(t_rows, cycle, live, row_gap, col_gap):
    denom = row_gap[:, None] + col_gap[None, :]
    update = jnp.where(live[:, None], cycle / denom, jnp.zeros_like(cycle))
    return t_rows.astype(jnp.float32) + update


def shards(packed_w, packed_t, row_energy, col_energy, block_order):
    ndev = lax.axis_size("dev")
    rank = lax.axis_index("dev")
    group = lax.axis_index("grp")
    local = packed_t.shape[1]
    true_rows = jnp.arange(local, dtype=jnp.int32) * ndev + rank
    blocks_w, blocks_t = (
        lax.all_to_all(packed_w, "grp", split_axis=0, concat_axis=2, tiled=True),
        lax.all_to_all(packed_t, "grp", split_axis=0, concat_axis=2, tiled=True),
    )
    w_rows = blocks_w[0]
    t_rows = blocks_t[0]
    order = lax.dynamic_index_in_dim(block_order, group, 0, keepdims=False)
    live = true_rows < order
    t_live = jnp.where(live[:, None], t_rows, jnp.zeros_like(t_rows))
    whole = lax.all_gather(t_live, "dev", axis=0, tiled=True)
    cycle = trimmed_product(w_rows, whole, order, ndev, local)
    new_block = apply_update(t_rows, cycle, live, row_energy[0], col_energy[0])
    return lax.all_to_all(new_block[None], "grp", split_axis=2, concat_axis=0, tiled=True)


def solution(mesh):
    in_specs = (P(None, "dev", "grp"), P(None, "dev", "grp"), P("grp", "dev"), P("grp", None), P())
    out_specs = P(None, "dev", "grp")
    return jax.shard_map(shards, mesh=mesh, in_specs=in_specs, out_specs=out_specs, check_vma=False)
```

profile of v0, /device:TPU:0, one launch (start us, length us, event | category | flops | bytes accessed | tf_op | source)
XLA Modules:
  0.0 218.4 jit_solution(17708460904780032008)
XLA Ops:
  6.5 0.0 copy-start.2
  6.5 5.5 %all-to-all-start = ((bf16[4,256,384]{2,1,0:T(8,128)(2,1)}), bf16[4,256,384]{2,1,0:T(8,128)(2,1)S(1)}, u32[]{:S(2)}, u32[]{:S(2)}) async-start(bf16[4,256,384]{2,1,0:T(8,128)(2,1)} %param.8), calls=%async_computation | async-start | bytes 1572864 | tf_op jit(solution)/shard_map/all_to_all | solution.py:38
  12.1 0.0 all-gather.2.cloned.1.call-start
  12.1 0.0 copy-done.2
  12.1 0.6 dynamic_slice.10
  12.7 0.6 add_compare_fusion
  13.3 11.1 %all-to-all-done = bf16[4,256,384]{2,1,0:T(8,128)(2,1)S(1)} async-done(((bf16[4,256,384]{2,1,0:T(8,128)(2,1)}), bf16[4,256,384]{2,1,0:T(8,128)(2,1)S(1)}, u32[]{:S(2)}, u32[]{:S(2)}) %all-to-all-start) | async-done | bytes 786464 | tf_op jit(solution)/shard_map/all_to_all | solution.py:38
  24.4 0.3 copy.14
  24.7 1.0 bitcast_select_fusion
  25.6 0.0 all-gather.2.cloned.1.call-update
  25.7 0.0 copy-start
  25.7 4.8 %all-to-all-start.1 = ((bf16[4,256,2048]{2,1,0:T(8,128)(2,1)}), bf16[4,256,2048]{2,1,0:T(8,128)(2,1)}, u32[]{:S(2)}, u32[]{:S(2)}) async-start(bf16[4,256,2048]{2,1,0:T(8,128)(2,1)} %param.7), calls=%async_computation.1 | async-start | bytes 8388608 | tf_op jit(solution)/shard_map/all_to_all | solution.py:37
  31.2 0.0 copy-done
  31.2 47.3 %all-to-all-done.1 = bf16[4,256,2048]{2,1,0:T(8,128)(2,1)} async-done(((bf16[4,256,2048]{2,1,0:T(8,128)(2,1)}), bf16[4,256,2048]{2,1,0:T(8,128)(2,1)}, u32[]{:S(2)}, u32[]{:S(2)}) %all-to-all-start.1) | async-done | bytes 4194336 | tf_op jit(solution)/shard_map/all_to_all | solution.py:37
  78.5 6.2 %copy.15 = bf16[1,256,4,2048]{1,3,2,0:T(8,128)(2,1)} copy(bf16[1,256,4,2048]{3,1,2,0:T(8,128)(2,1)} %bitcast.6) | data formatting | bytes 8388608 | tf_op jit(solution)/shard_map/all_to_all | solution.py:37
  84.7 42.4 %all-gather.2.cloned.1.call-done = bf16[8192,1536]{0,1:T(8,128)(2,1)} async-done(((bf16[256,1536]{0,1:T(8,128)(2,1)}), bf16[8192,1536]{0,1:T(8,128)(2,1)}) %all-gather.2.cloned.1.call-update) | async-done | bytes 25165840 | tf_op jit(solution)/shard_map/all_gather | solution.py:45
  127.1 32.6 %copy.20 = bf16[8192,1536]{1,0:T(8,128)(2,1)} copy(bf16[8192,1536]{0,1:T(8,128)(2,1)} %all-gather.2.cloned.1.call-done) | data formatting | bytes 50331648 | tf_op jit(solution)/shard_map/while | solution.py:21
  159.8 0.2 broadcast.17.clone
  160.0 19.9 %while.10 = (s32[]{:T(128)}, f32[256,1536]{1,0:T(8,128)S(1)}, s32[]{:T(128)}, bf16[256,32,256]{0,2,1:T(8,128)(2,1)}, bf16[32,256,1536]{2,1,0:T(8,128)(2,1)}, /*index=5*/s32[]{:T(128)}, s32[]{:T(128)}, s32[]{:T(128)}, s32[]{:T(128)}) while((s32[]{:T(128)}, f32[256,1536]{1,0:T(8,128)S(1)}, s32[]{:T(128)}, bf16[256,32,256]{0,2,1:T(8,128)(2,1)}, ...), condition=%wide.region_1.2_spmd, body=%wide.region_0.1_spmd.sunk | while | flops 1611005952 | bytes 10486923 | solution.py:21
  160.0 5.0 %fusion.15 = f32[256,1536]{1,0:T(8,128)S(1)} fusion(f32[256,1536]{1,0:T(8,128)S(1)} %get-tuple-element.96, bf16[32,256,1536]{2,1,0:T(8,128)(2,1)} %get-tuple-element.108, s32[]{:T(128)S(6)} %select_n.32, bf16[256,32,256]{0,2,1:T(8,128)(2,1)} %get-tuple-element.107), kind=kOutput, calls=%fused_computation.3.clone.1 | convolution fusion | flops 1611005952 | bytes 10486784 | tf_op jit(solution)/shard_map/while/body/pnb,nbc->pc/dot_general | solution.py:19
  165.0 5.0 %fusion.15 = f32[256,1536]{1,0:T(8,128)S(1)} fusion(f32[256,1536]{1,0:T(8,128)S(1)} %get-tuple-element.96, bf16[32,256,1536]{2,1,0:T(8,128)(2,1)} %get-tuple-element.108, s32[]{:T(128)S(6)} %select_n.32, bf16[256,32,256]{0,2,1:T(8,128)(2,1)} %get-tuple-element.107), kind=kOutput, calls=%fused_computation.3.clone.1 | convolution fusion | flops 1611005952 | bytes 10486784 | tf_op jit(solution)/shard_map/while/body/pnb,nbc->pc/dot_general | solution.py:19
  170.0 5.0 %fusion.15 = f32[256,1536]{1,0:T(8,128)S(1)} fusion(f32[256,1536]{1,0:T(8,128)S(1)} %get-tuple-element.96, bf16[32,256,1536]{2,1,0:T(8,128)(2,1)} %get-tuple-element.108, s32[]{:T(128)S(6)} %select_n.32, bf16[256,32,256]{0,2,1:T(8,128)(2,1)} %get-tuple-element.107), kind=kOutput, calls=%fused_computation.3.clone.1 | convolution fusion | flops 1611005952 | bytes 10486784 | tf_op jit(solution)/shard_map/while/body/pnb,nbc->pc/dot_general | solution.py:19
  174.9 5.0 %fusion.15 = f32[256,1536]{1,0:T(8,128)S(1)} fusion(f32[256,1536]{1,0:T(8,128)S(1)} %get-tuple-element.96, bf16[32,256,1536]{2,1,0:T(8,128)(2,1)} %get-tuple-element.108, s32[]{:T(128)S(6)} %select_n.32, bf16[256,32,256]{0,2,1:T(8,128)(2,1)} %get-tuple-element.107), kind=kOutput, calls=%fused_computation.3.clone.1 | convolution fusion | flops 1611005952 | bytes 10486784 | tf_op jit(solution)/shard_map/while/body/pnb,nbc->pc/dot_general | solution.py:19
  179.9 0.0 copy-start.1
  179.9 1.6 copy.18
  181.5 0.0 copy-done.1
  181.5 1.8 select_add_fusion
  183.3 1.1 broadcast_in_dim.24
  184.5 25.4 %all_to_all.48 = f32[1,256,1536]{1,0,2:T(1,128)S(1)} all-to-all(f32[1,256,1536]{1,0,2:T(1,128)S(1)} %broadcast_in_dim.24), channel_id=1, replica_groups=mesh['grp'=4,'dev'=32] {'grp'}, dimensions={2} | all-to-all | bytes 3145728 | tf_op jit(solution)/shard_map/all_to_all | solution.py:48
  209.8 0.1 copy.21
  209.9 1.6 copy.19
  (1 shorter events, 0.0 us)
Async XLA Ops:
  6.5 5.6 %copy-start.2 = (s32[4]{0:T(128)S(1)}, s32[4]{0:T(128)}, u32[]{:S(2)}) copy-start(s32[4]{0:T(128)} %param.11) | copy-start | bytes 52
  6.5 17.8 %all-to-all-start = ((bf16[4,256,384]{2,1,0:T(8,128)(2,1)}), bf16[4,256,384]{2,1,0:T(8,128)(2,1)S(1)}, u32[]{:S(2)}, u32[]{:S(2)}) async-start(bf16[4,256,384]{2,1,0:T(8,128)(2,1)} %param.8), calls=%async_computation | async-start | bytes 1572864 | tf_op jit(solution)/shard_map/all_to_all | solution.py:38
  12.1 115.1 %all-gather.2.cloned.1.call-start = ((), (), s32[]{:S(2)}) async-start(), calls=%async_computation.3 | async-start | bytes 25952256 | tf_op jit(solution)/shard_map/all_gather | solution.py:45
  25.7 5.5 %copy-start = (f32[1,1536]{1,0:T(1,128)S(1)}, f32[1,1536]{1,0:T(1,128)}, u32[]{:S(2)}) copy-start(f32[1,1536]{1,0:T(1,128)} %param.10) | copy-start | bytes 18436
  25.7 52.9 %all-to-all-start.1 = ((bf16[4,256,2048]{2,1,0:T(8,128)(2,1)}), bf16[4,256,2048]{2,1,0:T(8,128)(2,1)}, u32[]{:S(2)}, u32[]{:S(2)}) async-start(bf16[4,256,2048]{2,1,0:T(8,128)(2,1)} %param.7), calls=%async_computation.1 | async-start | bytes 8388608 | tf_op jit(solution)/shard_map/all_to_all | solution.py:37
  179.9 1.6 copy-start.1
Sparse Core Ops, SparseCore 0:
  25.8 101.3 all-gather.1
where the time goes:
time: 220 us; the launch traced here: 218 us
  waiting for transfers between devices  101 us (46%)
  local copies, waits for them, and re-layouts  44.4 us (20%)
  blocking collectives  25.4 us (12%)
  matrix products  19.8 us (9%)
  between operations  14.1 us (6%)
  starting transfers between devices  10.4 us (5%)
  other arithmetic  3.43 us (2%)
    all_to_all x1, waiting for transfers between devices, shards(): lax.all_to_all(packed_w, 'grp', split_axis=0, concat_axis=2, tiled=True)  47.3 us
    all_gather x1, waiting for transfers between devices, shards(): whole = lax.all_gather(t_live, 'dev', axis=0, tiled=True)  42.4 us
    while x2, local copies, waits for them, and re-layouts, trimmed_product(): lax.fori_loop(0, turns, step_block, jnp.zeros((local, columns), jnp.float...  34.3 us
    all_to_all x1, blocking collectives, shards(): lax.all_to_all(new_block[None], 'grp', split_axis=2, concat_axis=0, tiled...  25.4 us
    dot_general x4, matrix products, step_block(): jnp.einsum('pnb,nbc->pc', part_w, part_t, preferred_element_type=jnp.floa...  19.8 us
    all_to_all x1, waiting for transfers between devices, shards(): lax.all_to_all(packed_t, 'grp', split_axis=0, concat_axis=2, tiled=True)  11.1 us
    all_to_all x1, local copies, waits for them, and re-layouts, shards(): lax.all_to_all(packed_w, 'grp', split_axis=0, concat_axis=2, tiled=True)  6.18 us
    all_to_all x1, starting transfers between devices, shards(): lax.all_to_all(packed_t, 'grp', split_axis=0, concat_axis=2, tiled=True)  5.55 us
  transfers between devices with their start and end apart: 3, of which 3 were waited for; matrix products, arithmetic and copies ran while one was open for 3% of the time, Pallas kernels for 0%

commit v1 on v0

v1 whole, which is shorter than its diff:
```python
import jax
import jax.numpy as jnp
from jax import lax
from jax.sharding import Mesh, NamedSharding, PartitionSpec as P


def apply_update(t_rows, cycle, live, row_gap, col_gap):
    denom = row_gap[:, None] + col_gap[None, :]
    update = jnp.where(live[:, None], cycle / denom, jnp.zeros_like(cycle))
    return t_rows.astype(jnp.float32) + update


def shards(packed_w, packed_t, row_energy, col_energy, block_order):
    nchip = lax.axis_size("chip")
    ncore = lax.axis_size("dc")
    rank = lax.axis_index("chip") * ncore + lax.axis_index("dc")
    group = lax.axis_index("grp")
    local = packed_t.shape[1]
    ndev = nchip * ncore
    true_rows = jnp.arange(local, dtype=jnp.int32) * ndev + rank
    t_rows = lax.all_to_all(packed_t, "grp", split_axis=0, concat_axis=2, tiled=True)[0]
    order = lax.dynamic_index_in_dim(block_order, group, 0, keepdims=False)
    live = true_rows < order
    t_live = jnp.where(live[:, None], t_rows, jnp.zeros_like(t_rows))
    t_half = lax.all_gather(t_live, "chip", axis=0, tiled=True)
    w_rows = lax.all_to_all(packed_w, "grp", split_axis=0, concat_axis=2, tiled=True)[0]
    w4 = w_rows.reshape(local, nchip, ncore, local)
    w_mine = lax.all_to_all(w4, "dc", split_axis=2, concat_axis=0, tiled=True)
    w_mine = w_mine.reshape(ncore * local, nchip * local)
    partial = jnp.dot(w_mine, t_half, preferred_element_type=jnp.float32)
    cycle = lax.psum_scatter(partial, "dc", scatter_dimension=0, tiled=True)
    new_block = apply_update(t_rows, cycle, live, row_energy[0], col_energy[0])
    return lax.all_to_all(new_block[None], "grp", split_axis=2, concat_axis=0, tiled=True)


def solution(mesh):
    ngrp, ndev = mesh.devices.shape
    ncore = 2
    split = Mesh(mesh.devices.reshape(ngrp, ndev // ncore, ncore), ("grp", "chip", "dc"))
    rows = ("chip", "dc")
    in_specs = (P(None, rows, "grp"), P(None, rows, "grp"), P("grp", rows), P("grp", None), P())
    out_specs = P(None, rows, "grp")
    body = jax.shard_map(shards, mesh=split, in_specs=in_specs, out_specs=out_specs, check_vma=False)
    target = NamedSharding(mesh, P(None, "dev", "grp"))

    def run(*args):
        return lax.with_sharding_constraint(body(*args), target)

    return run
```

time: 220 us -> 193 us (0.88)
  waiting for transfers between devices: 101 us -> 40.2 us
  blocking collectives: 25.4 us -> 85.2 us
  local copies, waits for them, and re-layouts: 44.4 us -> 32.3 us
  matrix products: 19.8 us -> 12.1 us
  starting transfers between devices: 10.4 us -> 5.46 us
    all_to_all x0 -> x2, blocking collectives: none -> 59.9 us  [the longest x1 51.7 us: shards(): lax.all_to_all(packed_w, 'grp', split_axis=0, concat_axis=2, tiled=True)[0]]
    all_to_all x2 -> x1, waiting for transfers between devices: 58.4 us -> 10.4 us  [shards(): lax.all_to_all(packed_t, 'grp', split_axis=0, concat_axis=2, tiled=True)[0]]
    while x2 -> x0, local copies, waits for them, and re-layouts: 34.3 us -> none  [trimmed_product(): lax.fori_loop(0, turns, step_block, jnp.zeros((local, columns), jnp.float...]
    all_gather x1, waiting for transfers between devices: 42.4 us -> 17.2 us  [shards(): t_half = lax.all_gather(t_live, 'chip', axis=0, tiled=True)]
    unnamed x7 -> x6, local copies, waits for them, and re-layouts: 0.12 us -> 13.2 us
    reduce_scatter x0 -> x1, waiting for transfers between devices: none -> 12.6 us  [shards(): cycle = lax.psum_scatter(partial, 'dc', scatter_dimension=0, tiled=True)]
    dot_general x4 -> x1, matrix products: 19.8 us -> 12.1 us  [shards(): partial = jnp.dot(w_mine, t_half, preferred_element_type=jnp.float32)]
    broadcast_in_dim x1, local copies, waits for them, and re-layouts: 1.14 us -> 6.46 us  [shards(): new_block[None]]
  transfers between devices with their start and end apart: 3 -> 3, of which waited for: 3 -> 3; matrix products, arithmetic and copies ran while one was open for 3% -> 12% of each run, Pallas kernels for 0% -> 0%
where the time goes in v1:
time: 193 us; the launch traced here: 192 us
  blocking collectives  85.2 us (44%)
  waiting for transfers between devices  40.2 us (21%)
  local copies, waits for them, and re-layouts  32.3 us (17%)
  between operations  13.4 us (7%)
  matrix products  12.1 us (6%)
  starting transfers between devices  5.46 us (3%)
  other arithmetic  3.45 us (2%)
    all_to_all x1, blocking collectives, shards(): lax.all_to_all(packed_w, 'grp', split_axis=0, concat_axis=2, tiled=True)[0]  51.7 us
    all_to_all x1, blocking collectives, shards(): lax.all_to_all(new_block[None], 'grp', split_axis=2, concat_axis=0, tiled...  25.3 us
    all_gather x1, waiting for transfers between devices, shards(): t_half = lax.all_gather(t_live, 'chip', axis=0, tiled=True)  17.2 us
    unnamed x6, local copies, waits for them, and re-layouts  13.2 us
    reduce_scatter x1, waiting for transfers between devices, shards(): cycle = lax.psum_scatter(partial, 'dc', scatter_dimension=0, tiled=True)  12.6 us
    dot_general x1, matrix products, shards(): partial = jnp.dot(w_mine, t_half, preferred_element_type=jnp.float32)  12.1 us
    all_to_all x1, waiting for transfers between devices, shards(): lax.all_to_all(packed_t, 'grp', split_axis=0, concat_axis=2, tiled=True)[0]  10.4 us
    all_to_all x1, blocking collectives, shards(): w_mine = lax.all_to_all(w4, 'dc', split_axis=2, concat_axis=0, tiled=True)  8.16 us
  transfers between devices with their start and end apart: 3, of which 3 were waited for; matrix products, arithmetic and copies ran while one was open for 12% of the time, Pallas kernels for 0%

profile of v1, /device:TPU:0, one launch (start us, length us, event | category | flops | bytes accessed | tf_op | source)
XLA Modules:
  0.0 192.1 jit_solution(3250268429148516764)
XLA Ops:
  6.5 5.4 %all-to-all-start = ((bf16[4,256,384]{2,1,0:T(8,128)(2,1)}), bf16[4,256,384]{2,1,0:T(8,128)(2,1)S(1)}, u32[]{:S(2)}, u32[]{:S(2)}) async-start(bf16[4,256,384]{2,1,0:T(8,128)(2,1)} %param.6), calls=%async_computation | async-start | bytes 1572864 | tf_op jit(solution)/shard_map/all_to_all | solution.py:21
  12.0 0.0 all-gather.2.cloned.1.call-start
  12.0 1.2 dynamic_slice.4
  13.2 0.7 add_compare_fusion
  13.8 10.4 %all-to-all-done = bf16[4,256,384]{2,1,0:T(8,128)(2,1)S(1)} async-done(((bf16[4,256,384]{2,1,0:T(8,128)(2,1)}), bf16[4,256,384]{2,1,0:T(8,128)(2,1)S(1)}, u32[]{:S(2)}, u32[]{:S(2)}) %all-to-all-start) | async-done | bytes 786464 | tf_op jit(solution)/shard_map/all_to_all | solution.py:21
  24.2 0.3 copy.12
  24.5 1.0 bitcast_select_fusion
  25.5 0.0 all-gather.2.cloned.1.call-update
  25.5 0.0 reduce-scatter.2.cloned.1.call-start
  25.6 6.2 %copy.13 = bf16[4,256,2048]{1,2,0:T(8,128)(2,1)} copy(bf16[4,256,2048]{2,1,0:T(8,128)(2,1)} %param.5) | data formatting | bytes 8388608 | tf_op args[0]
  31.8 51.7 %all_to_all.63 = bf16[4,256,2048]{1,2,0:T(8,128)(2,1)S(1)} all-to-all(bf16[4,256,2048]{1,2,0:T(8,128)(2,1)} %copy.13), channel_id=1, replica_groups=mesh['grp'=4,'chip'=16,'dc'=2] {'grp'}, dimensions={0} | all-to-all | bytes 8388608 | tf_op jit(solution)/shard_map/all_to_all | solution.py:26
  83.5 0.4 copy.14
  83.9 8.2 %all_to_all.64 = bf16[256,16,2,256]{0,3,1,2:T(8,128)(2,1)} all-to-all(bf16[256,16,2,256]{0,3,1,2:T(8,128)(2,1)S(1)} %copy.14), channel_id=1, replica_groups=mesh['grp'=4,'chip'=16,'dc'=2] {'dc'}, dimensions={2} | all-to-all | bytes 8388608 | tf_op jit(solution)/shard_map/all_to_all | solution.py:28
  92.1 7.9 %copy.15 = bf16[2,256,16,1,256]{4,2,1,0,3:T(8,128)(2,1)} copy(bf16[2,256,16,1,256]{1,4,2,0,3:T(8,128)(2,1)} %bitcast.31) | data formatting | bytes 8388608 | tf_op jit(solution)/shard_map/all_to_all | solution.py:28
  100.0 6.3 %copy.18 = bf16[64,8,16,256]{3,1,2,0:T(8,128)(2,1)} copy(bf16[64,8,16,256]{3,2,1,0:T(8,128)(2,1)} %bitcast.32) | data formatting | bytes 8388608
  106.4 17.2 %all-gather.2.cloned.1.call-done = bf16[4096,1536]{0,1:T(8,128)(2,1)} async-done(((bf16[256,1536]{0,1:T(8,128)(2,1)}), bf16[4096,1536]{0,1:T(8,128)(2,1)}) %all-gather.2.cloned.1.call-update) | async-done | bytes 12582928 | tf_op jit(solution)/shard_map/all_gather | solution.py:25
  123.5 12.1 %convolution_bitcast_fusion = f32[512,1536]{0,1:T(8,128)} fusion(bf16[4096,1536]{0,1:T(8,128)(2,1)} %all-gather.2.cloned.1.call-done, bf16[512,4096]{1,0:T(8,128)(2,1)} %bitcast.34), kind=kOutput, calls=%fused_computation | convolution fusion | flops 6442450944 | bytes 19922944 | tf_op jit(solution)/shard_map/dot_general | solution.py:30
  135.6 0.0 copy-start
  135.6 0.0 copy-start.1
  135.6 0.0 reduce-scatter.2.cloned.1.call-update
  135.6 0.7 copy-done
  136.3 12.6 %reduce-scatter.2.cloned.1.call-done = f32[256,1536]{0,1:T(8,128)} async-done(((f32[512,1536]{0,1:T(8,128)}), f32[256,1536]{0,1:T(8,128)}) %reduce-scatter.2.cloned.1.call-update) | async-done | bytes 1572880 | tf_op jit(solution)/shard_map/reduce_scatter | solution.py:31
  148.9 0.0 copy-done.1
  148.9 1.8 add_bitcast_fusion
  150.7 6.5 %copy.16 = f32[1,256,1536]{1,0,2:T(1,128)S(1)} copy(f32[1,256,1536]{1,2,0:T(8,128)S(1)} %add_bitcast_fusion) | data formatting | bytes 3145728 | tf_op jit(solution)/shard_map/broadcast_in_dim | solution.py:33
  157.2 25.3 %all_to_all.65 = f32[1,256,1536]{1,0,2:T(1,128)S(1)} all-to-all(f32[1,256,1536]{1,0,2:T(1,128)S(1)} %copy.16), channel_id=1, replica_groups=mesh['grp'=4,'chip'=16,'dc'=2] {'grp'}, dimensions={2} | all-to-all | bytes 3145728 | tf_op jit(solution)/shard_map/all_to_all | solution.py:33
  182.5 2.7 %copy.17 = f32[1,256,4,384]{3,1,2,0:T(8,128)} copy(f32[1,256,4,384]{1,0,3,2:T(1,128)S(1)} %bitcast.33) | data formatting | bytes 3145728 | tf_op jit(solution)/shard_map/all_to_all | solution.py:33
  (1 shorter events, 0.0 us)
Async XLA Ops:
  6.5 17.7 %all-to-all-start = ((bf16[4,256,384]{2,1,0:T(8,128)(2,1)}), bf16[4,256,384]{2,1,0:T(8,128)(2,1)S(1)}, u32[]{:S(2)}, u32[]{:S(2)}) async-start(bf16[4,256,384]{2,1,0:T(8,128)(2,1)} %param.6), calls=%async_computation | async-start | bytes 1572864 | tf_op jit(solution)/shard_map/all_to_all | solution.py:21
  12.0 111.6 %all-gather.2.cloned.1.call-start = ((), (), s32[]{:S(2)}) async-start(), calls=%async_computation.5 | async-start | bytes 13369344 | tf_op jit(solution)/shard_map/all_gather | solution.py:25
  25.5 123.4 %reduce-scatter.2.cloned.1.call-start = ((), (), s32[]{:S(2)}) async-start(), calls=%async_computation.6 | async-start | bytes 4718592 | tf_op jit(solution)/shard_map/reduce_scatter | solution.py:31
  135.6 0.7 copy-start
  135.6 13.3 %copy-start.1 = (f32[1,256]{1,0:T(1,128)S(1)}, f32[1,256]{1,0:T(1,128)}, u32[]{:S(2)}) copy-start(f32[1,256]{1,0:T(1,128)} %param.7) | copy-start | bytes 3076
Sparse Core Ops, SparseCore 0:
  25.7 97.8 all-gather.1
  135.7 13.1 reduce-scatter.1

commit v2 on v1

v2 whole, which is shorter than its diff:
```python
import jax
import jax.numpy as jnp
from jax import lax
from jax.sharding import Mesh, NamedSharding, PartitionSpec as P


def apply_update(t_rows, cycle, live, row_gap, col_gap):
    denom = row_gap[:, None] + col_gap[None, :]
    update = jnp.where(live[:, None], cycle / denom, jnp.zeros_like(cycle))
    return t_rows.astype(jnp.float32) + update


def shift(x, axis, step):
    n = lax.axis_size(axis)
    return lax.ppermute(x, axis, [(i, (i + step) % n) for i in range(n)])


def ring4(x, axis):
    from_left = shift(x, axis, 1)
    from_right = shift(x, axis, -1)
    half = x.shape[0] // 2
    far_lo = shift(from_left[:half], axis, 1)
    far_hi = shift(from_right[half:], axis, -1)
    far = jnp.concatenate([far_lo, far_hi], axis=0)
    return jnp.stack([x, from_right, far, from_left], axis=0)


def shards(packed_w, packed_t, row_energy, col_energy, block_order):
    nx = lax.axis_size("dx")
    ny = lax.axis_size("dy")
    ncore = lax.axis_size("dc")
    ngrp = lax.axis_size("grp")
    x = lax.axis_index("dx")
    y = lax.axis_index("dy")
    c = lax.axis_index("dc")
    z = lax.axis_index("grp")
    rank = (x * ny + y) * ncore + c
    local = packed_t.shape[1]
    ndev = nx * ny * ncore
    true_rows = jnp.arange(local, dtype=jnp.int32) * ndev + rank

    t_rows = lax.all_to_all(packed_t, "grp", split_axis=0, concat_axis=2, tiled=True)[0]
    order = lax.dynamic_index_in_dim(block_order, z, 0, keepdims=False)
    live = true_rows < order
    t_live = jnp.where(live[:, None], t_rows, jnp.zeros_like(t_rows))

    half = local // 2
    col_a = ring4(t_live[:half], "dy")
    row_b = ring4(t_live[half:], "dx")
    all_a = ring4(col_a, "dx")
    all_b = ring4(row_b, "dy")

    cols = packed_w.shape[2] // (ny * ncore)
    w5 = packed_w.reshape(ngrp, local, ny, ncore, cols)
    w_c = lax.all_to_all(w5, "dc", split_axis=3, concat_axis=1, tiled=True)
    w_c = w_c.reshape(ngrp, ncore * local, ny, cols)
    got = [lax.dynamic_index_in_dim(w_c, z, 0, keepdims=False)]
    for s in range(1, ngrp):
        part = lax.dynamic_index_in_dim(w_c, (z + s) % ngrp, 0, keepdims=False)
        got.append(shift(part, "grp", s))
    w_s = jnp.stack(got, axis=0)
    ox = jnp.arange(nx, dtype=jnp.int32)
    oy = jnp.arange(ny, dtype=jnp.int32)
    s_of = (z - x - ox) % ngrp
    y_of = (y + oy) % ny
    w_rel = w_s[s_of][:, :, y_of]
    w_a = jnp.transpose(w_rel[..., :half], (1, 0, 2, 3)).reshape(ncore * local, -1)
    w_b = jnp.transpose(w_rel[..., half:], (1, 2, 0, 3)).reshape(ncore * local, -1)
    ncol = t_live.shape[1]
    partial = jnp.dot(w_a, all_a.reshape(-1, ncol), preferred_element_type=jnp.float32)
    partial = partial + jnp.dot(w_b, all_b.reshape(-1, ncol), preferred_element_type=jnp.float32)

    other = lax.dynamic_slice_in_dim(partial, (1 - c) * local, local, 0)
    mine = lax.dynamic_slice_in_dim(partial, c * local, local, 0)
    cycle = mine + shift(other, "dc", 1)
    new_block = apply_update(t_rows, cycle, live, row_energy[0], col_energy[0])
    return lax.all_to_all(new_block[None], "grp", split_axis=2, concat_axis=0, tiled=True)


def solution(mesh):
    ngrp, ndev = mesh.devices.shape
    ncore = 2
    nx = 4
    ny = ndev // (ncore * nx)
    split = Mesh(mesh.devices.reshape(ngrp, nx, ny, ncore), ("grp", "dx", "dy", "dc"))
    rows = ("dx", "dy", "dc")
    in_specs = (P(None, rows, "grp"), P(None, rows, "grp"), P("grp", rows), P("grp", None), P())
    out_specs = P(None, rows, "grp")
    body = jax.shard_map(shards, mesh=split, in_specs=in_specs, out_specs=out_specs, check_vma=False)
    target = NamedSharding(mesh, P(None, "dev", "grp"))

    def run(*args):
        return lax.with_sharding_constraint(body(*args), target)

    return run
```

time: 193 us -> 267 us (1.38)
  waiting for transfers between devices: 40.2 us -> 113 us
  blocking collectives: 85.2 us -> 25 us
  starting transfers between devices: 5.46 us -> 41.3 us
  local copies, waits for them, and re-layouts: 32.3 us -> 62.8 us
  between operations: 13.4 us -> 0.32 us
  other arithmetic: 3.45 us -> 13.5 us
    ppermute x0 -> x20, waiting for transfers between devices: none -> 97.1 us  [shift(): return lax.ppermute(x, axis, [(i, (i + step) % n) for i in range(n)])]
    all_to_all x2 -> x0, blocking collectives: 59.9 us -> none  [the longest x1 51.7 us: shards(): lax.all_to_all(packed_w, 'grp', split_axis=0, concat_axis=2, tiled=True)[0]]
    ppermute x0 -> x20, starting transfers between devices: none -> 30.1 us  [shift(): return lax.ppermute(x, axis, [(i, (i + step) % n) for i in range(n)])]
    gather x0 -> x4, local copies, waits for them, and re-layouts: none -> 24.6 us  [shards(): w_rel = w_s[s_of][:, :, y_of]]
    all_gather x1 -> x0, waiting for transfers between devices: 17.2 us -> none  [shards(): t_half = lax.all_gather(t_live, 'chip', axis=0, tiled=True)]
    reduce_scatter x1 -> x0, waiting for transfers between devices: 12.6 us -> none  [shards(): cycle = lax.psum_scatter(partial, 'dc', scatter_dimension=0, tiled=True)]
    another operation x0 -> x7, other arithmetic: none -> 10.3 us  [the longest x6 6.62 us: ring4(): return jnp.stack([x, from_right, far, from_left], axis=0)]
    slice x0 -> x8, local copies, waits for them, and re-layouts: none -> 7.55 us  [the longest x4 4.12 us: ring4(): far_hi = shift(from_right[half:], axis, -1)]
  transfers between devices with their start and end apart: 3 -> 22, of which waited for: 3 -> 9; matrix products, arithmetic and copies ran while one was open for 12% -> 26% of each run, Pallas kernels for 0% -> 0%
where the time goes in v2:
time: 267 us; the launch traced here: 266 us
  waiting for transfers between devices  113 us (42%)
  local copies, waits for them, and re-layouts  62.8 us (24%)
  starting transfers between devices  41.3 us (15%)
  blocking collectives  25 us (9%)
  other arithmetic  13.5 us (5%)
  matrix products  10.7 us (4%)
    ppermute x20, waiting for transfers between devices, shift(): return lax.ppermute(x, axis, [(i, (i + step) % n) for i in range(n)])  97.1 us
    ppermute x20, starting transfers between devices, shift(): return lax.ppermute(x, axis, [(i, (i + step) % n) for i in range(n)])  30.1 us
    all_to_all x1, blocking collectives, shards(): lax.all_to_all(new_block[None], 'grp', split_axis=2, concat_axis=0, tiled...  25 us
    gather x4, local copies, waits for them, and re-layouts, shards(): w_rel = w_s[s_of][:, :, y_of]  24.6 us
    all_to_all x1, waiting for transfers between devices, shards(): lax.all_to_all(packed_t, 'grp', split_axis=0, concat_axis=2, tiled=True)[0]  11 us
    unnamed x26, local copies, waits for them, and re-layouts  8.27 us
    all_to_all x1, local copies, waits for them, and re-layouts, shards(): w_c = lax.all_to_all(w5, 'dc', split_axis=3, concat_axis=1, tiled=True)  7.26 us
    another operation x6, other arithmetic, ring4(): return jnp.stack([x, from_right, far, from_left], axis=0)  6.62 us
  transfers between devices with their start and end apart: 22, of which 9 were waited for; matrix products, arithmetic and copies ran while one was open for 26% of the time, Pallas kernels for 0%

profile of v2, /device:TPU:0, one launch (start us, length us, event | category | flops | bytes accessed | tf_op | source)
XLA Modules:
  0.0 266.2 jit_solution(10579144242687021854)
XLA Ops:
  0.0 5.5 %all-to-all-start = ((bf16[4,256,384]{2,1,0:T(8,128)(2,1)}), bf16[4,256,384]{2,1,0:T(8,128)(2,1)S(1)}, u32[]{:S(2)}, u32[]{:S(2)}) async-start(bf16[4,256,384]{2,1,0:T(8,128)(2,1)} %param.6), calls=%async_computation | async-start | bytes 1572864 | tf_op jit(solution)/shard_map/all_to_all | solution.py:42
  6.8 11.0 %all-to-all-done = bf16[4,256,384]{2,1,0:T(8,128)(2,1)S(1)} async-done(((bf16[4,256,384]{2,1,0:T(8,128)(2,1)}), bf16[4,256,384]{2,1,0:T(8,128)(2,1)S(1)}, u32[]{:S(2)}, u32[]{:S(2)}) %all-to-all-start) | async-done | bytes 786464 | tf_op jit(solution)/shard_map/all_to_all | solution.py:42
  22.1 7.7 %collective-permute-done.12 = bf16[128,1536]{1,0:T(8,128)(2,1)S(1)} collective-permute-done((bf16[128,1536]{1,0:T(8,128)(2,1)S(1)}, bf16[128,1536]{1,0:T(8,128)(2,1)S(1)}, u32[]{:S(2)}, u32[]{:S(2)}) %collective-permute-start.12) | collective-permute-done | bytes 393248 | tf_op jit(solution)/shard_map/ppermute | solution.py:15
  30.2 3.0 %collective-permute-start.14 = (bf16[64,1536]{1,0:T(8,128)(2,1)S(1)}, bf16[64,1536]{1,0:T(8,128)(2,1)S(1)}, u32[]{:S(2)}, u32[]{:S(2)}) collective-permute-start(bf16[64,1536]{1,0:T(8,128)(2,1)S(1)} %slice.61), channel_id=1, source_target_pairs={{0,24},{8,0},{16,8},{24,16},{1,25},{9,1},{17,9},{25,17},{2,26},{10... | collective-permute-start | bytes 589832 | tf_op jit(solution)/shard_map/ppermute | solution.py:15
  33.2 3.6 %collective-permute-done.13 = bf16[64,1536]{1,0:T(8,128)(2,1)S(1)} collective-permute-done((bf16[64,1536]{1,0:T(8,128)(2,1)S(1)}, bf16[64,1536]{1,0:T(8,128)(2,1)S(1)}, u32[]{:S(2)}, u32[]{:S(2)}) %collective-permute-start.13) | collective-permute-done | bytes 196640 | tf_op jit(solution)/shard_map/ppermute | solution.py:15
  42.4 2.9 %collective-permute-start.3 = (bf16[128,1536]{1,0:T(8,128)(2,1)S(1)}, bf16[128,1536]{1,0:T(8,128)(2,1)S(1)}, u32[]{:S(2)}, u32[]{:S(2)}) collective-permute-start(bf16[128,1536]{1,0:T(8,128)(2,1)S(1)} %get-tuple-element.16), channel_id=1, source_target_pairs={{0,6},{2,0},{4,2},{6,4},{1,7},{3,1},{5,3},{7,5},{8,14},{10,8},{12,... | collective-permute-start | bytes 1179656 | tf_op jit(solution)/shard_map/ppermute | solution.py:15
  45.2 36.5 %collective-permute-done.4 = bf16[128,1536]{1,0:T(8,128)(2,1)S(1)} collective-permute-done((bf16[128,1536]{1,0:T(8,128)(2,1)S(1)}, bf16[128,1536]{1,0:T(8,128)(2,1)S(1)}, u32[]{:S(2)}, u32[]{:S(2)}) %collective-permute-start.4) | collective-permute-done | bytes 393248 | tf_op jit(solution)/shard_map/ppermute | solution.py:15
  85.8 6.2 %copy.21 = bf16[4,256,2048]{1,2,0:T(8,128)(2,1)} copy(bf16[4,256,2048]{2,1,0:T(8,128)(2,1)} %param.5) | data formatting | bytes 8388608 | tf_op args[0]
  92.0 4.6 %copy.22 = bf16[4,256,4,2,256]{1,4,2,0,3:T(8,128)(2,1)} copy(bf16[4,256,4,2,256]{1,4,3,2,0:T(8,128)(2,1)} %bitcast.76) | data formatting | bytes 8388608 | tf_op jit(solution)/shard_map/reshape | solution.py:54
  96.6 5.6 %all-to-all-start.1 = ((bf16[4,256,4,2,256]{1,4,2,0,3:T(8,128)(2,1)}), bf16[4,256,4,2,256]{1,4,2,0,3:T(8,128)(2,1)}, u32[]{:S(2)}, u32[]{:S(2)}) async-start(bf16[4,256,4,2,256]{1,4,2,0,3:T(8,128)(2,1)} %copy.22), calls=%async_computation.1 | async-start | bytes 8388608 | tf_op jit(solution)/shard_map/all_to_all | solution.py:55
  102.3 4.4 %all-to-all-done.1 = bf16[4,256,4,2,256]{1,4,2,0,3:T(8,128)(2,1)} async-done(((bf16[4,256,4,2,256]{1,4,2,0,3:T(8,128)(2,1)}), bf16[4,256,4,2,256]{1,4,2,0,3:T(8,128)(2,1)}, u32[]{:S(2)}, u32[]{:S(2)}) %all-to-all-start.1) | async-done | bytes 4194336 | tf_op jit(solution)/shard_map/all_to_all | solution.py:55
  106.8 7.3 %copy.23 = bf16[4,256,4,2,256]{4,1,3,2,0:T(8,128)(2,1)} copy(bf16[4,256,4,2,256]{1,4,2,0,3:T(8,128)(2,1)} %all-to-all-done.1) | data formatting | bytes 8388608 | tf_op jit(solution)/shard_map/all_to_all | solution.py:55
  114.0 3.9 %constant_dynamic-slice_fusion.1 = (bf16[1,512,4,256]{3,1,2,0:T(8,128)(2,1)S(1)}, bf16[512,4,256]{2,0,1:T(8,128)(2,1)S(1)}, bf16[512,4,256]{2,0,1:T(8,128)(2,1)}, bf16[512,4,256]{2,0,1:T(8,128)(2,1)}) fusion(bf16[4,512,4,256]{3,1,2,0:T(8,128)(2,1)} %bitcast.75, s32[]{:T(128)S(6)} %select_n.88, s32[]{:T(128)S(6)} %select_n.94, s32[]{:T(128)S(6)} %select_n.92, ...), kind=kLoop, calls=%fused_computation.47 | loop fusion | bytes 8388624 | tf_op jit(solution)/shard_map/jit(dynamic_index_in_dim)/dynamic_slice | solution.py:57
  118.6 2.1 collective-permute-start.1
  123.7 3.3 %collective-permute-start.7 = (bf16[4,128,1536]{2,1,0:T(8,128)(2,1)}, bf16[4,128,1536]{2,1,0:T(8,128)(2,1)}, u32[]{:S(2)}, u32[]{:S(2)}) collective-permute-start(bf16[4,128,1536]{2,1,0:T(8,128)(2,1)} %get-tuple-element.10), channel_id=1, source_target_pairs={{0,24},{8,0},{16,8},{24,16},{1,25},{9,1},{17,9},{25,17},{2,26},{10... | collective-permute-start | bytes 4718600 | tf_op jit(solution)/shard_map/ppermute | solution.py:15
  127.8 2.1 slice.62
  131.9 35.3 %collective-permute-done = bf16[512,4,256]{2,0,1:T(8,128)(2,1)} collective-permute-done((bf16[512,4,256]{2,0,1:T(8,128)(2,1)}, bf16[512,4,256]{2,0,1:T(8,128)(2,1)}, u32[]{:S(2)}, u32[]{:S(2)}) %collective-permute-start) | collective-permute-done | bytes 1048608 | tf_op jit(solution)/shard_map/ppermute | solution.py:15
  167.5 2.9 %collective-permute-start.18 = (bf16[2,128,1536]{2,1,0:T(8,128)(2,1)}, bf16[2,128,1536]{2,1,0:T(8,128)(2,1)}, u32[]{:S(2)}, u32[]{:S(2)}) collective-permute-start(bf16[2,128,1536]{2,1,0:T(8,128)(2,1)} %slice.63), channel_id=1, source_target_pairs={{0,6},{2,0},{4,2},{6,4},{1,7},{3,1},{5,3},{7,5},{8,14},{10,8},{12,... | collective-permute-start | bytes 2359304 | tf_op jit(solution)/shard_map/ppermute | solution.py:15
  170.5 3.7 %pad_maximum_fusion = bf16[4,512,4,256]{3,1,2,0:T(8,128)(2,1)} fusion(bf16[1,512,4,256]{3,1,2,0:T(8,128)(2,1)} %bitcast.14, bf16[1,512,4,256]{3,1,2,0:T(8,128)(2,1)} %bitcast.12, bf16[1,512,4,256]{3,1,2,0:T(8,128)(2,1)} %bitcast.10, bf16[1,512,4,256]{3,1,2,0:T(8,128)(2,1)S(1)} %get-tuple-element.5), kind=kLoop, calls=%fused_computation.18 | loop fusion | flops 6291456 | bytes 8388608 | tf_op jit(solution)/shard_map/stack | solution.py:61
  174.2 5.0 %gather_fusion = bf16[4,512,4,256]{3,1,2,0:T(8,128)(2,1)} fusion(bf16[4,512,4,256]{3,1,2,0:T(8,128)(2,1)} %pad_maximum_fusion, s32[1024]{0:T(1024)S(1)} %pad_clamp_fusion.1), kind=kCustom, calls=%fused_computation | custom fusion | bytes 8388624 | tf_op jit(solution)/shard_map/gather | solution.py:66
  179.2 7.3 %copy.24 = bf16[4,512,4,256]{1,3,0,2:T(8,128)(2,1)} copy(bf16[4,512,4,256]{3,1,2,0:T(8,128)(2,1)} %gather_fusion) | data formatting | bytes 8388608 | tf_op jit(solution)/shard_map/gather | solution.py:66
  186.5 5.0 %gather_fusion.1 = bf16[4,4,512,256]{2,3,1,0:T(8,128)(2,1)} fusion(bf16[4,512,4,256]{1,3,0,2:T(8,128)(2,1)} %copy.24, s32[1024]{0:T(1024)S(1)} %pad_clamp_fusion), kind=kCustom, calls=%fused_computation.1 | custom fusion | bytes 8388624 | tf_op jit(solution)/shard_map/gather | solution.py:66
  191.5 7.3 %copy.25 = bf16[4,4,512,256]{3,2,0,1:T(8,128)(2,1)} copy(bf16[4,4,512,256]{2,3,1,0:T(8,128)(2,1)} %gather_fusion.1) | data formatting | bytes 8388608 | tf_op jit(solution)/shard_map/gather | solution.py:66
  200.1 3.4 %collective-permute-start.10 = (bf16[2,128,1536]{2,1,0:T(8,128)(2,1)S(1)}, bf16[2,128,1536]{2,1,0:T(8,128)(2,1)S(1)}, u32[]{:S(2)}, u32[]{:S(2)}) collective-permute-start(bf16[2,128,1536]{2,1,0:T(8,128)(2,1)S(1)} %slice.57), channel_id=1, source_target_pairs={{0,24},{8,0},{16,8},{24,16},{1,25},{9,1},{17,9},{25,17},{2,26},{10... | collective-permute-start | bytes 2359304 | tf_op jit(solution)/shard_map/ppermute | solution.py:15
  206.6 5.4 %fusion.16 = f32[512,1536]{1,0:T(8,128)S(1)} fusion(bf16[1,4,128,1536]{3,2,1,0:T(8,128)(2,1)} %bitcast.37, bf16[1,4,128,1536]{3,2,1,0:T(8,128)(2,1)S(1)} %maximum_bitcast_fusion.1, bf16[1,4,128,1536]{3,2,1,0:T(8,128)(2,1)} %bitcast.35, bf16[1,4,128,1536]{3,2,1,0:T(8,128)(2,1)S(1)} %copy-done.2, bf16[4,512,4,256]{3,1,2,0:T(8,128)(2,1)S(1)} %bitcast.80), kind=kOutput, calls=%fused_computation.19 | convolution fusion | flops 3230662656 | bytes 11534336 | tf_op jit(solution)/shard_map/dot_general | solution.py:71
  212.0 5.4 %collective-permute-done.10 = bf16[2,128,1536]{2,1,0:T(8,128)(2,1)S(1)} collective-permute-done((bf16[2,128,1536]{2,1,0:T(8,128)(2,1)S(1)}, bf16[2,128,1536]{2,1,0:T(8,128)(2,1)S(1)}, u32[]{:S(2)}, u32[]{:S(2)}) %collective-permute-start.10) | collective-permute-done | bytes 786464 | tf_op jit(solution)/shard_map/ppermute | solution.py:15
  217.4 5.0 %collective-permute-done.9 = bf16[2,128,1536]{2,1,0:T(8,128)(2,1)S(1)} collective-permute-done((bf16[2,128,1536]{2,1,0:T(8,128)(2,1)S(1)}, bf16[2,128,1536]{2,1,0:T(8,128)(2,1)S(1)}, u32[]{:S(2)}, u32[]{:S(2)}) %collective-permute-start.9) | collective-permute-done | bytes 786464 | tf_op jit(solution)/shard_map/ppermute | solution.py:15
  222.6 5.3 %fusion.22 = f32[512,1536]{1,0:T(8,128)S(1)} fusion(f32[512,1536]{1,0:T(8,128)S(1)} %fusion.16, bf16[1,4,128,1536]{3,2,1,0:T(8,128)(2,1)} %bitcast.26, bf16[1,4,128,1536]{3,2,1,0:T(8,128)(2,1)S(1)} %maximum_bitcast_fusion, bf16[1,4,128,1536]{3,2,1,0:T(8,128)(2,1)} %bitcast.24, bf16[1,4,128,1536]{3,2,1,0:T(8,128)(2,1)S(1)} %copy-done.3, ...), kind=kOutput, calls=%fused_computation.21 | convolution fusion | flops 3231449088 | bytes 14680064 | tf_op jit(solution)/shard_map/dot_general | solution.py:70
  230.1 3.6 %collective-permute-done.19 = f32[256,1536]{1,0:T(8,128)S(1)} collective-permute-done((f32[256,1536]{1,0:T(8,128)}, f32[256,1536]{1,0:T(8,128)S(1)}, u32[]{:S(2)}, u32[]{:S(2)}) %collective-permute-start.19) | collective-permute-done | bytes 1572896 | tf_op jit(solution)/shard_map/ppermute | solution.py:15
  234.9 2.4 add_bitcast_fusion
  238.5 25.0 %all_to_all.48 = f32[1,256,1536]{1,0,2:T(1,128)S(1)} all-to-all(f32[1,256,1536]{1,0,2:T(1,128)S(1)} %copy.27), channel_id=1, replica_groups=mesh['grp'=4,'dx'=4,'dy'=4,'dc'=2] {'grp'}, dimensions={2} | all-to-all | bytes 3145728 | tf_op jit(solution)/shard_map/all_to_all | solution.py:77
  263.5 2.7 %copy.28 = f32[1,256,4,384]{3,1,2,0:T(8,128)} copy(f32[1,256,4,384]{1,0,3,2:T(1,128)S(1)} %bitcast.79) | data formatting | bytes 3145728 | tf_op jit(solution)/shard_map/all_to_all | solution.py:77
  (77 shorter events, 31.3 us)
Async XLA Ops:
  0.0 5.6 %copy-start.11 = (s32[4]{0:T(128)S(1)}, s32[4]{0:T(128)}, u32[]{:S(2)}) copy-start(s32[4]{0:T(128)} %param.9) | copy-start | bytes 52
  0.0 17.8 %all-to-all-start = ((bf16[4,256,384]{2,1,0:T(8,128)(2,1)}), bf16[4,256,384]{2,1,0:T(8,128)(2,1)S(1)}, u32[]{:S(2)}, u32[]{:S(2)}) async-start(bf16[4,256,384]{2,1,0:T(8,128)(2,1)} %param.6), calls=%async_computation | async-start | bytes 1572864 | tf_op jit(solution)/shard_map/all_to_all | solution.py:42
  18.8 11.0 %collective-permute-start.12 = (bf16[128,1536]{1,0:T(8,128)(2,1)S(1)}, bf16[128,1536]{1,0:T(8,128)(2,1)S(1)}, u32[]{:S(2)}, u32[]{:S(2)}) collective-permute-start(bf16[128,1536]{1,0:T(8,128)(2,1)S(1)} %get-tuple-element.15), channel_id=1, source_target_pairs={{0,8},{8,16},{16,24},{24,0},{1,9},{9,17},{17,25},{25,1},{2,10},{10... | collective-permute-start | bytes 1179656 | tf_op jit(solution)/shard_map/ppermute | solution.py:15
  20.4 9.8 %collective-permute-start.11 = (bf16[128,1536]{1,0:T(8,128)(2,1)S(1)}, bf16[128,1536]{1,0:T(8,128)(2,1)S(1)}, u32[]{:S(2)}, u32[]{:S(2)}) collective-permute-start(bf16[128,1536]{1,0:T(8,128)(2,1)S(1)} %get-tuple-element.15), channel_id=1, source_target_pairs={{0,24},{8,0},{16,8},{24,16},{1,25},{9,1},{17,9},{25,17},{2,26},{10... | collective-permute-start | bytes 1179656 | tf_op jit(solution)/shard_map/ppermute | solution.py:15
  29.8 6.9 %collective-permute-start.13 = (bf16[64,1536]{1,0:T(8,128)(2,1)S(1)}, bf16[64,1536]{1,0:T(8,128)(2,1)S(1)}, u32[]{:S(2)}, u32[]{:S(2)}) collective-permute-start(bf16[64,1536]{1,0:T(8,128)(2,1)S(1)} %slice.60), channel_id=1, source_target_pairs={{0,8},{8,16},{16,24},{24,0},{1,9},{9,17},{17,25},{25,1},{2,10},{10... | collective-permute-start | bytes 589832 | tf_op jit(solution)/shard_map/ppermute | solution.py:15
  30.2 6.6 %collective-permute-start.14 = (bf16[64,1536]{1,0:T(8,128)(2,1)S(1)}, bf16[64,1536]{1,0:T(8,128)(2,1)S(1)}, u32[]{:S(2)}, u32[]{:S(2)}) collective-permute-start(bf16[64,1536]{1,0:T(8,128)(2,1)S(1)} %slice.61), channel_id=1, source_target_pairs={{0,24},{8,0},{16,8},{24,16},{1,25},{9,1},{17,9},{25,17},{2,26},{10... | collective-permute-start | bytes 589832 | tf_op jit(solution)/shard_map/ppermute | solution.py:15
  38.8 88.3 %collective-permute-start.16 = (bf16[4,128,1536]{2,1,0:T(8,128)(2,1)}, bf16[4,128,1536]{2,1,0:T(8,128)(2,1)}, u32[]{:S(2)}, u32[]{:S(2)}) collective-permute-start(bf16[4,128,1536]{2,1,0:T(8,128)(2,1)} %get-tuple-element.12), channel_id=1, source_target_pairs={{0,2},{2,4},{4,6},{6,0},{1,3},{3,5},{5,7},{7,1},{8,10},{10,12},{12... | collective-permute-start | bytes 4718600 | tf_op jit(solution)/shard_map/ppermute | solution.py:15
  40.3 86.7 %collective-permute-start.15 = (bf16[4,128,1536]{2,1,0:T(8,128)(2,1)}, bf16[4,128,1536]{2,1,0:T(8,128)(2,1)}, u32[]{:S(2)}, u32[]{:S(2)}) collective-permute-start(bf16[4,128,1536]{2,1,0:T(8,128)(2,1)} %get-tuple-element.12), channel_id=1, source_target_pairs={{0,6},{2,0},{4,2},{6,4},{1,7},{3,1},{5,3},{7,5},{8,14},{10,8},{12,... | collective-permute-start | bytes 4718600 | tf_op jit(solution)/shard_map/ppermute | solution.py:15
  42.0 39.8 %collective-permute-start.4 = (bf16[128,1536]{1,0:T(8,128)(2,1)S(1)}, bf16[128,1536]{1,0:T(8,128)(2,1)S(1)}, u32[]{:S(2)}, u32[]{:S(2)}) collective-permute-start(bf16[128,1536]{1,0:T(8,128)(2,1)S(1)} %get-tuple-element.16), channel_id=1, source_target_pairs={{0,2},{2,4},{4,6},{6,0},{1,3},{3,5},{5,7},{7,1},{8,10},{10,12},{12... | collective-permute-start | bytes 1179656 | tf_op jit(solution)/shard_map/ppermute | solution.py:15
  42.4 41.0 %collective-permute-start.3 = (bf16[128,1536]{1,0:T(8,128)(2,1)S(1)}, bf16[128,1536]{1,0:T(8,128)(2,1)S(1)}, u32[]{:S(2)}, u32[]{:S(2)}) collective-permute-start(bf16[128,1536]{1,0:T(8,128)(2,1)S(1)} %get-tuple-element.16), channel_id=1, source_target_pairs={{0,6},{2,0},{4,2},{6,4},{1,7},{3,1},{5,3},{7,5},{8,14},{10,8},{12,... | collective-permute-start | bytes 1179656 | tf_op jit(solution)/shard_map/ppermute | solution.py:15
  81.8 10.3 %copy-start.5 = (bf16[128,1536]{1,0:T(8,128)(2,1)}, bf16[128,1536]{1,0:T(8,128)(2,1)S(1)}, u32[]{:S(2)}) copy-start(bf16[128,1536]{1,0:T(8,128)(2,1)S(1)} %collective-permute-done.4) | copy-start | bytes 1179652
  81.8 36.8 %collective-permute-start.5 = (bf16[64,1536]{1,0:T(8,128)(2,1)S(1)}, bf16[64,1536]{1,0:T(8,128)(2,1)}, u32[]{:S(2)}, u32[]{:S(2)}) collective-permute-start(bf16[64,1536]{1,0:T(8,128)(2,1)S(1)} %slice.54), channel_id=1, source_target_pairs={{0,2},{2,4},{4,6},{6,0},{1,3},{3,5},{5,7},{7,1},{8,10},{10,12},{12... | collective-permute-start | bytes 589832 | tf_op jit(solution)/shard_map/ppermute | solution.py:15
  83.4 8.7 %copy-start.7 = (bf16[128,1536]{1,0:T(8,128)(2,1)}, bf16[128,1536]{1,0:T(8,128)(2,1)S(1)}, u32[]{:S(2)}) copy-start(bf16[128,1536]{1,0:T(8,128)(2,1)S(1)} %collective-permute-done.3) | copy-start | bytes 1179652
  84.1 36.5 %collective-permute-start.6 = (bf16[64,1536]{1,0:T(8,128)(2,1)}, bf16[64,1536]{1,0:T(8,128)(2,1)}, u32[]{:S(2)}, u32[]{:S(2)}) collective-permute-start(bf16[64,1536]{1,0:T(8,128)(2,1)} %slice.55), channel_id=1, source_target_pairs={{0,6},{2,0},{4,2},{6,4},{1,7},{3,1},{5,3},{7,5},{8,14},{10,8},{12,... | collective-permute-start | bytes 589832 | tf_op jit(solution)/shard_map/ppermute | solution.py:15
  96.6 10.1 %all-to-all-start.1 = ((bf16[4,256,4,2,256]{1,4,2,0,3:T(8,128)(2,1)}), bf16[4,256,4,2,256]{1,4,2,0,3:T(8,128)(2,1)}, u32[]{:S(2)}, u32[]{:S(2)}) async-start(bf16[4,256,4,2,256]{1,4,2,0,3:T(8,128)(2,1)} %copy.22), calls=%async_computation.1 | async-start | bytes 8388608 | tf_op jit(solution)/shard_map/all_to_all | solution.py:55
  114.0 7.6 %copy-start.6 = (bf16[128,1536]{1,0:T(8,128)(2,1)S(1)}, bf16[128,1536]{1,0:T(8,128)(2,1)}, u32[]{:S(2)}) copy-start(bf16[128,1536]{1,0:T(8,128)(2,1)} %copy-done.5) | copy-start | bytes 1179652
  114.0 7.7 %copy-start.8 = (bf16[128,1536]{1,0:T(8,128)(2,1)S(1)}, bf16[128,1536]{1,0:T(8,128)(2,1)}, u32[]{:S(2)}) copy-start(bf16[128,1536]{1,0:T(8,128)(2,1)} %copy-done.7) | copy-start | bytes 1179652
  118.0 49.2 %collective-permute-start = (bf16[512,4,256]{2,0,1:T(8,128)(2,1)}, bf16[512,4,256]{2,0,1:T(8,128)(2,1)}, u32[]{:S(2)}, u32[]{:S(2)}) collective-permute-start(bf16[512,4,256]{2,0,1:T(8,128)(2,1)} %get-tuple-element.8), channel_id=1, source_target_pairs={{0,32},{32,64},{64,96},{96,0},{1,33},{33,65},{65,97},{97,1},{2,34}... | collective-permute-start | bytes 3145736 | tf_op jit(solution)/shard_map/ppermute | solution.py:15
  118.6 49.0 %collective-permute-start.1 = (bf16[512,4,256]{2,0,1:T(8,128)(2,1)}, bf16[512,4,256]{2,0,1:T(8,128)(2,1)}, u32[]{:S(2)}, u32[]{:S(2)}) collective-permute-start(bf16[512,4,256]{2,0,1:T(8,128)(2,1)} %get-tuple-element.7), channel_id=1, source_target_pairs={{0,64},{32,96},{64,0},{96,32},{1,65},{33,97},{65,1},{97,33},{2,66}... | collective-permute-start | bytes 3145736 | tf_op jit(solution)/shard_map/ppermute | solution.py:15
  123.7 75.1 %collective-permute-start.7 = (bf16[4,128,1536]{2,1,0:T(8,128)(2,1)}, bf16[4,128,1536]{2,1,0:T(8,128)(2,1)}, u32[]{:S(2)}, u32[]{:S(2)}) collective-permute-start(bf16[4,128,1536]{2,1,0:T(8,128)(2,1)} %get-tuple-element.10), channel_id=1, source_target_pairs={{0,24},{8,0},{16,8},{24,16},{1,25},{9,1},{17,9},{25,17},{2,26},{10... | collective-permute-start | bytes 4718600 | tf_op jit(solution)/shard_map/ppermute | solution.py:15
  127.0 76.5 %collective-permute-start.8 = (bf16[4,128,1536]{2,1,0:T(8,128)(2,1)}, bf16[4,128,1536]{2,1,0:T(8,128)(2,1)}, u32[]{:S(2)}, u32[]{:S(2)}) collective-permute-start(bf16[4,128,1536]{2,1,0:T(8,128)(2,1)} %get-tuple-element.10), channel_id=1, source_target_pairs={{0,8},{8,16},{16,24},{24,0},{1,9},{9,17},{17,25},{25,1},{2,10},{10... | collective-permute-start | bytes 4718600 | tf_op jit(solution)/shard_map/ppermute | solution.py:15
  127.0 43.5 %collective-permute-start.2 = (bf16[512,4,256]{2,0,1:T(8,128)(2,1)S(1)}, bf16[512,4,256]{2,0,1:T(8,128)(2,1)}, u32[]{:S(2)}, u32[]{:S(2)}) collective-permute-start(bf16[512,4,256]{2,0,1:T(8,128)(2,1)S(1)} %get-tuple-element.6), channel_id=1, source_target_pairs={{0,96},{32,0},{64,32},{96,64},{1,97},{33,1},{65,33},{97,65},{2,98}... | collective-permute-start | bytes 3145736 | tf_op jit(solution)/shard_map/ppermute | solution.py:15
  167.2 37.9 %collective-permute-start.17 = (bf16[2,128,1536]{2,1,0:T(8,128)(2,1)}, bf16[2,128,1536]{2,1,0:T(8,128)(2,1)}, u32[]{:S(2)}, u32[]{:S(2)}) collective-permute-start(bf16[2,128,1536]{2,1,0:T(8,128)(2,1)} %slice.62), channel_id=1, source_target_pairs={{0,2},{2,4},{4,6},{6,0},{1,3},{3,5},{5,7},{7,1},{8,10},{10,12},{12... | collective-permute-start | bytes 2359304 | tf_op jit(solution)/shard_map/ppermute | solution.py:15
  167.5 37.6 %collective-permute-start.18 = (bf16[2,128,1536]{2,1,0:T(8,128)(2,1)}, bf16[2,128,1536]{2,1,0:T(8,128)(2,1)}, u32[]{:S(2)}, u32[]{:S(2)}) collective-permute-start(bf16[2,128,1536]{2,1,0:T(8,128)(2,1)} %slice.63), channel_id=1, source_target_pairs={{0,6},{2,0},{4,2},{6,4},{1,7},{3,1},{5,3},{7,5},{8,14},{10,8},{12,... | collective-permute-start | bytes 2359304 | tf_op jit(solution)/shard_map/ppermute | solution.py:15
  198.8 7.8 %copy-start.2 = (bf16[1,4,128,1536]{3,2,1,0:T(8,128)(2,1)S(1)}, bf16[1,4,128,1536]{3,2,1,0:T(8,128)(2,1)}, u32[]{:S(2)}) copy-start(bf16[1,4,128,1536]{3,2,1,0:T(8,128)(2,1)} %get-tuple-element.11) | copy-start | bytes 4718596
  200.1 17.4 %collective-permute-start.10 = (bf16[2,128,1536]{2,1,0:T(8,128)(2,1)S(1)}, bf16[2,128,1536]{2,1,0:T(8,128)(2,1)S(1)}, u32[]{:S(2)}, u32[]{:S(2)}) collective-permute-start(bf16[2,128,1536]{2,1,0:T(8,128)(2,1)S(1)} %slice.57), channel_id=1, source_target_pairs={{0,24},{8,0},{16,8},{24,16},{1,25},{9,1},{17,9},{25,17},{2,26},{10... | collective-permute-start | bytes 2359304 | tf_op jit(solution)/shard_map/ppermute | solution.py:15
  203.5 3.1 %copy-start = (bf16[4,4,512,256]{3,2,0,1:T(8,128)(2,1)S(1)}, bf16[4,4,512,256]{3,2,0,1:T(8,128)(2,1)}, u32[]{:S(2)}) copy-start(bf16[4,4,512,256]{3,2,0,1:T(8,128)(2,1)} %copy.25) | copy-start | bytes 12582916
  204.8 17.6 %collective-permute-start.9 = (bf16[2,128,1536]{2,1,0:T(8,128)(2,1)S(1)}, bf16[2,128,1536]{2,1,0:T(8,128)(2,1)S(1)}, u32[]{:S(2)}, u32[]{:S(2)}) collective-permute-start(bf16[2,128,1536]{2,1,0:T(8,128)(2,1)S(1)} %slice.56), channel_id=1, source_target_pairs={{0,8},{8,16},{16,24},{24,0},{1,9},{9,17},{17,25},{25,1},{2,10},{10... | collective-permute-start | bytes 2359304 | tf_op jit(solution)/shard_map/ppermute | solution.py:15
  212.0 10.6 %copy-start.3 = (bf16[1,4,128,1536]{3,2,1,0:T(8,128)(2,1)S(1)}, bf16[1,4,128,1536]{3,2,1,0:T(8,128)(2,1)}, u32[]{:S(2)}) copy-start(bf16[1,4,128,1536]{3,2,1,0:T(8,128)(2,1)} %get-tuple-element.9) | copy-start | bytes 4718596
  227.9 2.2 copy-start.1
  228.0 6.9 %copy-start.10 = (f32[1,256]{1,0:T(1,128)S(1)}, f32[1,256]{1,0:T(1,128)}, u32[]{:S(2)}) copy-start(f32[1,256]{1,0:T(1,128)} %param.7) | copy-start | bytes 3076
  230.1 3.6 %collective-permute-start.19 = (f32[256,1536]{1,0:T(8,128)}, f32[256,1536]{1,0:T(8,128)S(1)}, u32[]{:S(2)}, u32[]{:S(2)}) collective-permute-start(f32[256,1536]{1,0:T(8,128)} %constant_dynamic-slice_fusion), channel_id=1, source_target_pairs={{0,1},{1,0},{2,3},{3,2},{4,5},{5,4},{6,7},{7,6},{8,9},{9,8},{10,11... | collective-permute-start | bytes 4718600 | tf_op jit(solution)/shard_map/ppermute | solution.py:15
  (2 other events, 3.3 us)

commit v3 on v2

v3 whole, which is shorter than its diff:
```python
import jax
import jax.numpy as jnp
from jax import lax
from jax.sharding import Mesh, NamedSharding, PartitionSpec as P


def apply_update(t_rows, cycle, live, row_gap, col_gap):
    denom = row_gap[:, None] + col_gap[None, :]
    update = jnp.where(live[:, None], cycle / denom, jnp.zeros_like(cycle))
    return t_rows.astype(jnp.float32) + update


def shift(x, axis, step):
    n = lax.axis_size(axis)
    return lax.ppermute(x, axis, [(i, (i + step) % n) for i in range(n)])


def place(buf, piece, index, axis):
    start = [0] * buf.ndim
    start[axis] = index
    return lax.dynamic_update_slice(buf, jnp.expand_dims(piece, axis), start)


def ring4(x, axis, me, buf, buf_axis):
    n = lax.axis_size(axis)
    from_left = shift(x, axis, 1)
    from_right = shift(x, axis, -1)
    half = x.shape[0] // 2
    far_lo = shift(from_left[:half], axis, 1)
    far_hi = shift(from_right[half:], axis, -1)
    buf = place(buf, x, me, buf_axis)
    buf = place(buf, from_left, (me + n - 1) % n, buf_axis)
    buf = place(buf, from_right, (me + 1) % n, buf_axis)
    far = (me + 2) % n
    lo = [0] * buf.ndim
    lo[buf_axis] = far
    buf = lax.dynamic_update_slice(buf, jnp.expand_dims(far_lo, buf_axis), lo)
    hi = list(lo)
    hi[buf_axis + 1] = half
    buf = lax.dynamic_update_slice(buf, jnp.expand_dims(far_hi, buf_axis), hi)
    return buf


def shards(packed_w, packed_t, row_energy, col_energy, block_order):
    nx = lax.axis_size("dx")
    ny = lax.axis_size("dy")
    ncore = lax.axis_size("dc")
    ngrp = lax.axis_size("grp")
    x = lax.axis_index("dx")
    y = lax.axis_index("dy")
    c = lax.axis_index("dc")
    z = lax.axis_index("grp")
    rank = (x * ny + y) * ncore + c
    local = packed_t.shape[1]
    ndev = nx * ny * ncore
    true_rows = jnp.arange(local, dtype=jnp.int32) * ndev + rank

    t_rows = lax.all_to_all(packed_t, "grp", split_axis=0, concat_axis=2, tiled=True)[0]
    order = lax.dynamic_index_in_dim(block_order, z, 0, keepdims=False)
    live = true_rows < order
    t_live = jnp.where(live[:, None], t_rows, jnp.zeros_like(t_rows))
    ncol = t_live.shape[1]

    half = local // 2
    col_a = ring4(t_live[:half], "dy", y, jnp.zeros((ny, half, ncol), t_live.dtype), 0)
    row_b = ring4(t_live[half:], "dx", x, jnp.zeros((nx, half, ncol), t_live.dtype), 0)
    t_abs = jnp.zeros((nx, ny, local, ncol), t_live.dtype)
    t_abs = ring4(col_a, "dx", x, t_abs[:, :, :half], 0)
    t_b = ring4(row_b, "dy", y, jnp.zeros((ny, nx, half, ncol), t_live.dtype), 0)
    t_abs = jnp.concatenate([t_abs, jnp.transpose(t_b, (1, 0, 2, 3))], axis=2)

    cols = packed_w.shape[2] // (ny * ncore)
    wv = packed_w.reshape(ngrp, local, ny, ncore, cols)
    w_own = jnp.zeros((local, nx, ny, cols), packed_w.dtype)
    w_oth = jnp.zeros((local, nx, ny, cols), packed_w.dtype)
    for sz in range(ngrp):
        for sc in range(ncore):
            piece = wv[(z + sz) % ngrp, :, :, (c + sc) % ncore, :]
            if sz or sc:
                n = ngrp * ncore
                perm = []
                for i in range(n):
                    gi, ci = divmod(i, ncore)
                    perm.append((i, ((gi + sz) % ngrp) * ncore + (ci + sc) % ncore))
                piece = lax.ppermute(piece, ("grp", "dc"), perm)
            where = (z - sz) % ngrp
            if sc:
                w_oth = place(w_oth, piece, where, 1)
            else:
                w_own = place(w_own, piece, where, 1)

    t_flat = t_abs.reshape(-1, ncol)
    mine = jnp.dot(w_own.reshape(local, -1), t_flat, preferred_element_type=jnp.float32)
    other = jnp.dot(w_oth.reshape(local, -1), t_flat, preferred_element_type=jnp.float32)
    cycle = mine + shift(other, "dc", 1)
    new_block = apply_update(t_rows, cycle, live, row_energy[0], col_energy[0])
    return lax.all_to_all(new_block[None], "grp", split_axis=2, concat_axis=0, tiled=True)


def solution(mesh):
    ngrp, ndev = mesh.devices.shape
    ncore = 2
    nx = 4
    ny = ndev // (ncore * nx)
    split = Mesh(mesh.devices.reshape(ngrp, nx, ny, ncore), ("grp", "dx", "dy", "dc"))
    rows = ("dx", "dy", "dc")
    in_specs = (P(None, rows, "grp"), P(None, rows, "grp"), P("grp", rows), P("grp", None), P())
    out_specs = P(None, rows, "grp")
    body = jax.shard_map(shards, mesh=split, in_specs=in_specs, out_specs=out_specs, check_vma=False)
    target = NamedSharding(mesh, P(None, "dev", "grp"))

    def run(*args):
        return lax.with_sharding_constraint(body(*args), target)

    return run
```

time: 267 us -> 218 us (0.82)
  waiting for transfers between devices: 113 us -> 69.3 us
  other arithmetic: 13.5 us -> 0.84 us
  starting transfers between devices: 41.3 us -> 48.9 us
  local copies, waits for them, and re-layouts: 62.8 us -> 56.2 us
  matrix products: 10.7 us -> 16.2 us
    ppermute x20 -> x17, waiting for transfers between devices: 97.1 us -> 47.6 us  [shift(): return lax.ppermute(x, axis, [(i, (i + step) % n) for i in range(n)])]
    gather x4 -> x0, local copies, waits for them, and re-layouts: 24.6 us -> none  [shards(): w_rel = w_s[s_of][:, :, y_of]]
    ppermute x0 -> x7, starting transfers between devices: none -> 16.5 us  [shards(): piece = lax.ppermute(piece, ('grp', 'dc'), perm)]
    ppermute x0 -> x7, waiting for transfers between devices: none -> 15.9 us  [shards(): piece = lax.ppermute(piece, ('grp', 'dc'), perm)]
    dynamic_slice x2 -> x8, local copies, waits for them, and re-layouts: 5.3 us -> 20.2 us  [shards(): piece = wv[(z + sz) % ngrp, :, :, (c + sc) % ncore, :]]
    dynamic_update_slice x0 -> x28, local copies, waits for them, and re-layouts: none -> 14.6 us  [the longest x20 14.3 us: place(): return lax.dynamic_update_slice(buf, jnp.expand_dims(piece, axis), start)]
    another operation x7 -> x0, other arithmetic: 10.3 us -> none  [the longest x6 6.62 us: ring4(): return jnp.stack([x, from_right, far, from_left], axis=0)]
    unnamed x26 -> x19, local copies, waits for them, and re-layouts: 8.27 us -> 0.14 us
  transfers between devices with their start and end apart: 22 -> 25, of which waited for: 9 -> 10; matrix products, arithmetic and copies ran while one was open for 26% -> 13% of each run, Pallas kernels for 0% -> 0%
where the time goes in v3:
time: 218 us; the launch traced here: 217 us
  waiting for transfers between devices  69.3 us (32%)
  local copies, waits for them, and re-layouts  56.2 us (26%)
  starting transfers between devices  48.9 us (22%)
  blocking collectives  25.3 us (12%)
  matrix products  16.2 us (7%)
    ppermute x17, waiting for transfers between devices, shift(): return lax.ppermute(x, axis, [(i, (i + step) % n) for i in range(n)])  47.6 us
    ppermute x17, starting transfers between devices, shift(): return lax.ppermute(x, axis, [(i, (i + step) % n) for i in range(n)])  27.5 us
    all_to_all x1, blocking collectives, shards(): lax.all_to_all(new_block[None], 'grp', split_axis=2, concat_axis=0, tiled...  25.3 us
    dynamic_slice x8, local copies, waits for them, and re-layouts, shards(): piece = wv[(z + sz) % ngrp, :, :, (c + sc) % ncore, :]  20.2 us
    ppermute x7, starting transfers between devices, shards(): piece = lax.ppermute(piece, ('grp', 'dc'), perm)  16.5 us
    ppermute x7, waiting for transfers between devices, shards(): piece = lax.ppermute(piece, ('grp', 'dc'), perm)  15.9 us
    dynamic_update_slice x20, local copies, waits for them, and re-layouts, place(): return lax.dynamic_update_slice(buf, jnp.expand_dims(piece, axis), start)  14.3 us
    dot_general x1, matrix products, shards(): jnp.dot(w_own.reshape(local, -1), t_flat, preferred_element_type=jnp.floa...  8.4 us
  transfers between devices with their start and end apart: 25, of which 10 were waited for; matrix products, arithmetic and copies ran while one was open for 13% of the time, Pallas kernels for 0%

profile of v3, /device:TPU:0, one launch (start us, length us, event | category | flops | bytes accessed | tf_op | source)
XLA Modules:
  0.0 217.2 jit_solution(18357853735116422822)
XLA Ops:
  0.0 7.8 %reshape.14 = bf16[4,256,4,2,256]{4,3,2,1,0:T(2,128)(2,1)} reshape(bf16[4,256,2048]{2,1,0:T(8,128)(2,1)} %param.5) | data formatting | bytes 8388608 | tf_op jit(solution)/shard_map/reshape | solution.py:73
  7.8 13.0 %constant_dynamic-slice_fusion.4 = (bf16[1,256,4,1,256]{4,3,2,1,0:T(2,128)(2,1)S(1)}, bf16[1,256,4,1,256]{4,3,2,1,0:T(2,128)(2,1)}, bf16[1,256,4,1,256]{4,3,2,1,...) fusion(bf16[4,256,4,2,256]{4,3,2,1,0:T(2,128)(2,1)} %reshape.14, ...), kind=kLoop, calls=%fused_computation.50 | loop fusion | bytes 8388632 | tf_op jit(solution)/shard_map/dynamic_slice | solution.py:78
  22.7 2.1 collective-permute-start.20
  24.8 4.9 %all-to-all-start = ((bf16[4,256,384]{2,1,0:T(8,128)(2,1)}), bf16[4,256,384]{2,1,0:T(8,128)(2,1)}, u32[]{:S(2)}, u32[]{:S(2)}) async-start(bf16[4,256,384]{2,1,0:T(8,128)(2,1)} %param.6), calls=%async_computation | async-start | bytes 1572864 | tf_op jit(solution)/shard_map/all_to_all | solution.py:58
  29.7 2.3 %copy.65 = bf16[1,256,4,1,256]{4,1,2,3,0:T(8,128)(2,1)} copy(bf16[1,256,4,1,256]{4,3,2,1,0:T(2,128)(2,1)} %get-tuple-element.7) | data formatting | bytes 1048576 | tf_op jit(solution)/shard_map/dynamic_slice | solution.py:78
  31.9 2.6 %collective-permute-start.21 = (bf16[256,4,256]{2,0,1:T(8,128)(2,1)}, bf16[256,4,256]{2,0,1:T(8,128)(2,1)}, u32[]{:S(2)}, u32[]{:S(2)}) collective-permute-start(bf16[256,4,256]{2,0,1:T(8,128)(2,1)} %bitcast.124), channel_id=1, source_target_pairs={{0,65},{1,64},{32,97},{33,96},{64,1},{65,0},{96,33},{97,32},{2,67}... | collective-permute-start | bytes 1572872 | tf_op jit(solution)/shard_map/ppermute | solution.py:85
  40.2 1.9 bitcast_dynamic-update-slice_fusion.13
  42.1 1.9 bitcast_dynamic-update-slice_fusion.12
  44.0 5.9 %all-to-all-done = bf16[4,256,384]{2,1,0:T(8,128)(2,1)} async-done(((bf16[4,256,384]{2,1,0:T(8,128)(2,1)}), bf16[4,256,384]{2,1,0:T(8,128)(2,1)}, u32[]{:S(2)}, u32[]{:S(2)}) %all-to-all-start) | async-done | bytes 786464 | tf_op jit(solution)/shard_map/all_to_all | solution.py:58
  57.1 6.0 %collective-permute-done.3 = bf16[128,1536]{1,0:T(8,128)(2,1)S(1)} collective-permute-done((bf16[128,1536]{1,0:T(8,128)(2,1)S(1)}, bf16[128,1536]{1,0:T(8,128)(2,1)S(1)}, u32[]{:S(2)}, u32[]{:S(2)}) %collective-permute-start.3) | collective-permute-done | bytes 393248 | tf_op jit(solution)/shard_map/ppermute | solution.py:15
  63.1 2.8 %collective-permute-start.12 = (bf16[128,1536]{1,0:T(8,128)(2,1)S(1)}, bf16[128,1536]{1,0:T(8,128)(2,1)S(1)}, u32[]{:S(2)}, u32[]{:S(2)}) collective-permute-start(bf16[128,1536]{1,0:T(8,128)(2,1)S(1)} %get-tuple-element.14), channel_id=1, source_target_pairs={{0,24},{8,0},{16,8},{24,16},{1,25},{9,1},{17,9},{25,17},{2,26},{10... | collective-permute-start | bytes 1179656 | tf_op jit(solution)/shard_map/ppermute | solution.py:15
  66.2 3.0 %collective-permute-start.6 = (bf16[64,1536]{1,0:T(8,128)(2,1)S(1)}, bf16[64,1536]{1,0:T(8,128)(2,1)S(1)}, u32[]{:S(2)}, u32[]{:S(2)}) collective-permute-start(bf16[64,1536]{1,0:T(8,128)(2,1)S(1)} %slice.42), channel_id=1, source_target_pairs={{0,6},{2,0},{4,2},{6,4},{1,7},{3,1},{5,3},{7,5},{8,14},{10,8},{12,... | collective-permute-start | bytes 589832 | tf_op jit(solution)/shard_map/ppermute | solution.py:15
  69.4 2.9 %collective-permute-done.12 = bf16[128,1536]{1,0:T(8,128)(2,1)S(1)} collective-permute-done((bf16[128,1536]{1,0:T(8,128)(2,1)S(1)}, bf16[128,1536]{1,0:T(8,128)(2,1)S(1)}, u32[]{:S(2)}, u32[]{:S(2)}) %collective-permute-start.12) | collective-permute-done | bytes 393248 | tf_op jit(solution)/shard_map/ppermute | solution.py:15
  73.6 2.7 %collective-permute-start.14 = (bf16[64,1536]{1,0:T(8,128)(2,1)S(1)}, bf16[64,1536]{1,0:T(8,128)(2,1)S(1)}, u32[]{:S(2)}, u32[]{:S(2)}) collective-permute-start(bf16[64,1536]{1,0:T(8,128)(2,1)S(1)} %slice.47), channel_id=1, source_target_pairs={{0,24},{8,0},{16,8},{24,16},{1,25},{9,1},{17,9},{25,17},{2,26},{10... | collective-permute-start | bytes 589832 | tf_op jit(solution)/shard_map/ppermute | solution.py:15
  76.5 5.3 %collective-permute-done.13 = bf16[64,1536]{1,0:T(8,128)(2,1)S(1)} collective-permute-done((bf16[64,1536]{1,0:T(8,128)(2,1)S(1)}, bf16[64,1536]{1,0:T(8,128)(2,1)S(1)}, u32[]{:S(2)}, u32[]{:S(2)}) %collective-permute-start.13) | collective-permute-done | bytes 196640 | tf_op jit(solution)/shard_map/ppermute | solution.py:15
  81.7 2.0 collective-permute-start.8
  84.2 2.9 %collective-permute-start.16 = (bf16[4,128,1536]{2,1,0:T(8,128)(2,1)S(1)}, bf16[4,128,1536]{2,1,0:T(8,128)(2,1)S(1)}, u32[]{:S(2)}, u32[]{:S(2)}) collective-permute-start(bf16[4,128,1536]{2,1,0:T(8,128)(2,1)S(1)} %bitcast_dynamic-update-slice_fusion.24), channel_id=1, source_target_pairs={{0,6},{2,0},{4,2},{6,4},{1,7},{3,1},{5,3},{7,5},{8,14},{10,8},{12,... | collective-permute-start | bytes 4718600 | tf_op jit(solution)/shard_map/ppermute | solution.py:15
  92.4 20.4 %collective-permute-done.7 = bf16[4,128,1536]{2,1,0:T(8,128)(2,1)S(1)} collective-permute-done((bf16[4,128,1536]{2,1,0:T(8,128)(2,1)S(1)}, bf16[4,128,1536]{2,1,0:T(8,128)(2,1)S(1)}, u32[]{:S(2)}, u32[]{:S(2)}) %collective-permute-start.7) | collective-permute-done | bytes 1572896 | tf_op jit(solution)/shard_map/ppermute | solution.py:15
  113.3 3.8 %collective-permute-start.10 = (bf16[2,128,1536]{2,1,0:T(8,128)(2,1)S(1)}, bf16[2,128,1536]{2,1,0:T(8,128)(2,1)S(1)}, u32[]{:S(2)}, u32[]{:S(2)}) collective-permute-start(bf16[2,128,1536]{2,1,0:T(8,128)(2,1)S(1)} %slice.44), channel_id=1, source_target_pairs={{0,24},{8,0},{16,8},{24,16},{1,25},{9,1},{17,9},{25,17},{2,26},{10... | collective-permute-start | bytes 2359304 | tf_op jit(solution)/shard_map/ppermute | solution.py:15
  117.6 3.0 %collective-permute-start.18 = (bf16[2,128,1536]{2,1,0:T(8,128)(2,1)S(1)}, bf16[2,128,1536]{2,1,0:T(8,128)(2,1)S(1)}, u32[]{:S(2)}, u32[]{:S(2)}) collective-permute-start(bf16[2,128,1536]{2,1,0:T(8,128)(2,1)S(1)} %slice.49), channel_id=1, source_target_pairs={{0,6},{2,0},{4,2},{6,4},{1,7},{3,1},{5,3},{7,5},{8,14},{10,8},{12,... | collective-permute-start | bytes 2359304 | tf_op jit(solution)/shard_map/ppermute | solution.py:15
  121.2 9.9 %collective-permute-done.9 = bf16[2,128,1536]{2,1,0:T(8,128)(2,1)S(1)} collective-permute-done((bf16[2,128,1536]{2,1,0:T(8,128)(2,1)S(1)}, bf16[2,128,1536]{2,1,0:T(8,128)(2,1)S(1)}, u32[]{:S(2)}, u32[]{:S(2)}) %collective-permute-start.9) | collective-permute-done | bytes 786464 | tf_op jit(solution)/shard_map/ppermute | solution.py:15
  131.3 2.8 %collective-permute-done.17 = bf16[2,128,1536]{2,1,0:T(8,128)(2,1)S(1)} collective-permute-done((bf16[2,128,1536]{2,1,0:T(8,128)(2,1)S(1)}, bf16[2,128,1536]{2,1,0:T(8,128)(2,1)S(1)}, u32[]{:S(2)}, u32[]{:S(2)}) %collective-permute-start.17) | collective-permute-done | bytes 786464 | tf_op jit(solution)/shard_map/ppermute | solution.py:15
  134.3 7.8 %fusion.4 = f32[256,1536]{1,0:T(8,128)} fusion(bf16[256,4,4,256]{3,0,2,1:T(8,128)(2,1)} %bitcast_dynamic-update-slice_fusion.10, bf16[4,4,128,1536]{3,2,1,0:T(8,128)(2,1)S(1)} %bitcast.130, bf16[4,4,128,1536]{3,2,0,1:T(8,128)(2,1)S(1)} %bitcast_dynamic-update-slice_fusion.7), kind=kOutput, calls=%fused_computation.5 | convolution fusion | flops 3246391296 | bytes 16252928 | tf_op jit(solution)/shard_map/dot_general | solution.py:94
  143.0 2.2 collective-permute-start
  146.2 5.2 %collective-permute-start.1 = (bf16[256,4,256]{2,0,1:T(8,128)(2,1)}, bf16[256,4,256]{2,0,1:T(8,128)(2,1)}, u32[]{:S(2)}, u32[]{:S(2)}) collective-permute-start(bf16[256,4,256]{2,0,1:T(8,128)(2,1)} %bitcast.128), channel_id=1, source_target_pairs={{0,64},{1,65},{32,96},{33,97},{64,0},{65,1},{96,32},{97,33},{2,66}... | collective-permute-start | bytes 1572872 | tf_op jit(solution)/shard_map/ppermute | solution.py:85
  151.5 2.7 %collective-permute-start.2 = (bf16[256,4,256]{2,0,1:T(8,128)(2,1)S(1)}, bf16[256,4,256]{2,0,1:T(8,128)(2,1)S(1)}, u32[]{:S(2)}, u32[]{:S(2)}) collective-permute-start(bf16[256,4,256]{2,0,1:T(8,128)(2,1)S(1)} %bitcast.136), channel_id=1, source_target_pairs={{0,96},{1,97},{32,0},{33,1},{64,32},{65,33},{96,64},{97,65},{2,98}... | collective-permute-start | bytes 1572872 | tf_op jit(solution)/shard_map/ppermute | solution.py:85
  156.7 2.1 collective-permute-done
  160.8 13.7 %collective-permute-done.1 = bf16[256,4,256]{2,0,1:T(8,128)(2,1)} collective-permute-done((bf16[256,4,256]{2,0,1:T(8,128)(2,1)}, bf16[256,4,256]{2,0,1:T(8,128)(2,1)}, u32[]{:S(2)}, u32[]{:S(2)}) %collective-permute-start.1) | collective-permute-done | bytes 524320 | tf_op jit(solution)/shard_map/ppermute | solution.py:85
  177.2 8.4 %fusion.8 = f32[1,256,1536]{2,1,0:T(8,128)} fusion(f32[256,1536]{1,0:T(8,128)} %collective-permute-done.23, bf16[256,4,4,256]{3,0,2,1:T(8,128)(2,1)} %bitcast_dynamic-update-slice_fusion.14, bf16[4,4,128,1536]{3,2,1,0:T(8,128)(2,1)} %bitcast.131, bf16[256,1536]{1,0:T(8,128)(2,1)S(1)} %bitcast.134, f32[1536]{0:T(1024)S(1)} %reduce, f32[256]{0:T(256)S(1)} %bitcast.137, ...), kind=kOutput, calls=%fused_computation.9 | convolution fusion | flops 3248750592 | bytes 18619648 | tf_op jit(solution)/shard_map/dot_general | solution.py:93
  185.6 3.6 %copy.45 = f32[1,256,1536]{1,0,2:T(1,128)S(1)} copy(f32[1,256,1536]{2,1,0:T(8,128)} %fusion.8) | data formatting | bytes 3145728 | tf_op jit(solution)/shard_map/broadcast_in_dim | solution.py:97
  189.2 25.3 %all_to_all.33 = f32[1,256,1536]{1,0,2:T(1,128)S(1)} all-to-all(f32[1,256,1536]{1,0,2:T(1,128)S(1)} %copy.45), channel_id=1, replica_groups=mesh['grp'=4,'dx'=4,'dy'=4,'dc'=2] {'grp'}, dimensions={2} | all-to-all | bytes 3145728 | tf_op jit(solution)/shard_map/all_to_all | solution.py:97
  214.4 2.7 %copy.46 = f32[1,256,4,384]{3,1,2,0:T(8,128)} copy(f32[1,256,4,384]{1,0,3,2:T(1,128)S(1)} %bitcast.132) | data formatting | bytes 3145728 | tf_op jit(solution)/shard_map/all_to_all | solution.py:97
  (99 shorter events, 33.3 us)
Async XLA Ops:
  21.8 16.9 %collective-permute-start.19 = (bf16[256,4,256]{2,0,1:T(8,128)(2,1)}, bf16[256,4,256]{2,0,1:T(8,128)(2,1)}, u32[]{:S(2)}, u32[]{:S(2)}) collective-permute-start(bf16[256,4,256]{2,0,1:T(8,128)(2,1)} %bitcast.126), channel_id=1, source_target_pairs={{0,1},{1,0},{32,33},{33,32},{64,65},{65,64},{96,97},{97,96},{2,3},... | collective-permute-start | bytes 1572872 | tf_op jit(solution)/shard_map/ppermute | solution.py:85
  22.7 19.4 %collective-permute-start.20 = (bf16[256,4,256]{2,0,1:T(8,128)(2,1)}, bf16[256,4,256]{2,0,1:T(8,128)(2,1)}, u32[]{:S(2)}, u32[]{:S(2)}) collective-permute-start(bf16[256,4,256]{2,0,1:T(8,128)(2,1)} %bitcast.125), channel_id=1, source_target_pairs={{0,33},{1,32},{32,65},{33,64},{64,97},{65,96},{96,1},{97,0},{2,35}... | collective-permute-start | bytes 1572872 | tf_op jit(solution)/shard_map/ppermute | solution.py:85
  24.8 25.1 %all-to-all-start = ((bf16[4,256,384]{2,1,0:T(8,128)(2,1)}), bf16[4,256,384]{2,1,0:T(8,128)(2,1)}, u32[]{:S(2)}, u32[]{:S(2)}) async-start(bf16[4,256,384]{2,1,0:T(8,128)(2,1)} %param.6), calls=%async_computation | async-start | bytes 1572864 | tf_op jit(solution)/shard_map/all_to_all | solution.py:58
  29.7 7.6 %copy-start.8 = (s32[4]{0:T(128)S(1)}, s32[4]{0:T(128)}, u32[]{:S(2)}) copy-start(s32[4]{0:T(128)} %param.9) | copy-start | bytes 52
  31.9 52.3 %collective-permute-start.21 = (bf16[256,4,256]{2,0,1:T(8,128)(2,1)}, bf16[256,4,256]{2,0,1:T(8,128)(2,1)}, u32[]{:S(2)}, u32[]{:S(2)}) collective-permute-start(bf16[256,4,256]{2,0,1:T(8,128)(2,1)} %bitcast.124), channel_id=1, source_target_pairs={{0,65},{1,64},{32,97},{33,96},{64,1},{65,0},{96,33},{97,32},{2,67}... | collective-permute-start | bytes 1572872 | tf_op jit(solution)/shard_map/ppermute | solution.py:85
  35.5 53.5 %collective-permute-start.22 = (bf16[256,4,256]{2,0,1:T(8,128)(2,1)}, bf16[256,4,256]{2,0,1:T(8,128)(2,1)}, u32[]{:S(2)}, u32[]{:S(2)}) collective-permute-start(bf16[256,4,256]{2,0,1:T(8,128)(2,1)} %bitcast.123), channel_id=1, source_target_pairs={{0,97},{1,96},{32,1},{33,0},{64,33},{65,32},{96,65},{97,64},{2,99}... | collective-permute-start | bytes 1572872 | tf_op jit(solution)/shard_map/ppermute | solution.py:85
  52.0 11.1 %collective-permute-start.3 = (bf16[128,1536]{1,0:T(8,128)(2,1)S(1)}, bf16[128,1536]{1,0:T(8,128)(2,1)S(1)}, u32[]{:S(2)}, u32[]{:S(2)}) collective-permute-start(bf16[128,1536]{1,0:T(8,128)(2,1)S(1)} %get-tuple-element.13), channel_id=1, source_target_pairs={{0,2},{2,4},{4,6},{6,0},{1,3},{3,5},{5,7},{7,1},{8,10},{10,12},{12... | collective-permute-start | bytes 1179656 | tf_op jit(solution)/shard_map/ppermute | solution.py:15
  53.6 12.2 %collective-permute-start.4 = (bf16[128,1536]{1,0:T(8,128)(2,1)S(1)}, bf16[128,1536]{1,0:T(8,128)(2,1)S(1)}, u32[]{:S(2)}, u32[]{:S(2)}) collective-permute-start(bf16[128,1536]{1,0:T(8,128)(2,1)S(1)} %get-tuple-element.13), channel_id=1, source_target_pairs={{0,6},{2,0},{4,2},{6,4},{1,7},{3,1},{5,3},{7,5},{8,14},{10,8},{12,... | collective-permute-start | bytes 1179656 | tf_op jit(solution)/shard_map/ppermute | solution.py:15
  55.3 11.0 %collective-permute-start.11 = (bf16[128,1536]{1,0:T(8,128)(2,1)S(1)}, bf16[128,1536]{1,0:T(8,128)(2,1)S(1)}, u32[]{:S(2)}, u32[]{:S(2)}) collective-permute-start(bf16[128,1536]{1,0:T(8,128)(2,1)S(1)} %get-tuple-element.14), channel_id=1, source_target_pairs={{0,8},{8,16},{16,24},{24,0},{1,9},{9,17},{17,25},{25,1},{2,10},{10... | collective-permute-start | bytes 1179656 | tf_op jit(solution)/shard_map/ppermute | solution.py:15
  63.1 9.2 %collective-permute-start.12 = (bf16[128,1536]{1,0:T(8,128)(2,1)S(1)}, bf16[128,1536]{1,0:T(8,128)(2,1)S(1)}, u32[]{:S(2)}, u32[]{:S(2)}) collective-permute-start(bf16[128,1536]{1,0:T(8,128)(2,1)S(1)} %get-tuple-element.14), channel_id=1, source_target_pairs={{0,24},{8,0},{16,8},{24,16},{1,25},{9,1},{17,9},{25,17},{2,26},{10... | collective-permute-start | bytes 1179656 | tf_op jit(solution)/shard_map/ppermute | solution.py:15
  65.8 7.7 %collective-permute-start.5 = (bf16[64,1536]{1,0:T(8,128)(2,1)S(1)}, bf16[64,1536]{1,0:T(8,128)(2,1)S(1)}, u32[]{:S(2)}, u32[]{:S(2)}) collective-permute-start(bf16[64,1536]{1,0:T(8,128)(2,1)S(1)} %slice.41), channel_id=1, source_target_pairs={{0,2},{2,4},{4,6},{6,0},{1,3},{3,5},{5,7},{7,1},{8,10},{10,12},{12... | collective-permute-start | bytes 589832 | tf_op jit(solution)/shard_map/ppermute | solution.py:15
  66.2 10.1 %collective-permute-start.6 = (bf16[64,1536]{1,0:T(8,128)(2,1)S(1)}, bf16[64,1536]{1,0:T(8,128)(2,1)S(1)}, u32[]{:S(2)}, u32[]{:S(2)}) collective-permute-start(bf16[64,1536]{1,0:T(8,128)(2,1)S(1)} %slice.42), channel_id=1, source_target_pairs={{0,6},{2,0},{4,2},{6,4},{1,7},{3,1},{5,3},{7,5},{8,14},{10,8},{12,... | collective-permute-start | bytes 589832 | tf_op jit(solution)/shard_map/ppermute | solution.py:15
  72.3 9.4 %collective-permute-start.13 = (bf16[64,1536]{1,0:T(8,128)(2,1)S(1)}, bf16[64,1536]{1,0:T(8,128)(2,1)S(1)}, u32[]{:S(2)}, u32[]{:S(2)}) collective-permute-start(bf16[64,1536]{1,0:T(8,128)(2,1)S(1)} %slice.46), channel_id=1, source_target_pairs={{0,8},{8,16},{16,24},{24,0},{1,9},{9,17},{17,25},{25,1},{2,10},{10... | collective-permute-start | bytes 589832 | tf_op jit(solution)/shard_map/ppermute | solution.py:15
  73.6 10.2 %collective-permute-start.14 = (bf16[64,1536]{1,0:T(8,128)(2,1)S(1)}, bf16[64,1536]{1,0:T(8,128)(2,1)S(1)}, u32[]{:S(2)}, u32[]{:S(2)}) collective-permute-start(bf16[64,1536]{1,0:T(8,128)(2,1)S(1)} %slice.47), channel_id=1, source_target_pairs={{0,24},{8,0},{16,8},{24,16},{1,25},{9,1},{17,9},{25,17},{2,26},{10... | collective-permute-start | bytes 589832 | tf_op jit(solution)/shard_map/ppermute | solution.py:15
  76.4 36.5 %collective-permute-start.7 = (bf16[4,128,1536]{2,1,0:T(8,128)(2,1)S(1)}, bf16[4,128,1536]{2,1,0:T(8,128)(2,1)S(1)}, u32[]{:S(2)}, u32[]{:S(2)}) collective-permute-start(bf16[4,128,1536]{2,1,0:T(8,128)(2,1)S(1)} %bitcast_dynamic-update-slice_fusion.26), channel_id=1, source_target_pairs={{0,8},{8,16},{16,24},{24,0},{1,9},{9,17},{17,25},{25,1},{2,10},{10... | collective-permute-start | bytes 4718600 | tf_op jit(solution)/shard_map/ppermute | solution.py:15
  81.7 31.5 %collective-permute-start.8 = (bf16[4,128,1536]{2,1,0:T(8,128)(2,1)S(1)}, bf16[4,128,1536]{2,1,0:T(8,128)(2,1)S(1)}, u32[]{:S(2)}, u32[]{:S(2)}) collective-permute-start(bf16[4,128,1536]{2,1,0:T(8,128)(2,1)S(1)} %bitcast_dynamic-update-slice_fusion.26), channel_id=1, source_target_pairs={{0,24},{8,0},{16,8},{24,16},{1,25},{9,1},{17,9},{25,17},{2,26},{10... | collective-permute-start | bytes 4718600 | tf_op jit(solution)/shard_map/ppermute | solution.py:15
  83.8 33.2 %collective-permute-start.15 = (bf16[4,128,1536]{2,1,0:T(8,128)(2,1)S(1)}, bf16[4,128,1536]{2,1,0:T(8,128)(2,1)S(1)}, u32[]{:S(2)}, u32[]{:S(2)}) collective-permute-start(bf16[4,128,1536]{2,1,0:T(8,128)(2,1)S(1)} %bitcast_dynamic-update-slice_fusion.24), channel_id=1, source_target_pairs={{0,2},{2,4},{4,6},{6,0},{1,3},{3,5},{5,7},{7,1},{8,10},{10,12},{12... | collective-permute-start | bytes 4718600 | tf_op jit(solution)/shard_map/ppermute | solution.py:15
  84.2 33.3 %collective-permute-start.16 = (bf16[4,128,1536]{2,1,0:T(8,128)(2,1)S(1)}, bf16[4,128,1536]{2,1,0:T(8,128)(2,1)S(1)}, u32[]{:S(2)}, u32[]{:S(2)}) collective-permute-start(bf16[4,128,1536]{2,1,0:T(8,128)(2,1)S(1)} %bitcast_dynamic-update-slice_fusion.24), channel_id=1, source_target_pairs={{0,6},{2,0},{4,2},{6,4},{1,7},{3,1},{5,3},{7,5},{8,14},{10,8},{12,... | collective-permute-start | bytes 4718600 | tf_op jit(solution)/shard_map/ppermute | solution.py:15
  112.9 18.3 %collective-permute-start.9 = (bf16[2,128,1536]{2,1,0:T(8,128)(2,1)S(1)}, bf16[2,128,1536]{2,1,0:T(8,128)(2,1)S(1)}, u32[]{:S(2)}, u32[]{:S(2)}) collective-permute-start(bf16[2,128,1536]{2,1,0:T(8,128)(2,1)S(1)} %slice.43), channel_id=1, source_target_pairs={{0,8},{8,16},{16,24},{24,0},{1,9},{9,17},{17,25},{25,1},{2,10},{10... | collective-permute-start | bytes 2359304 | tf_op jit(solution)/shard_map/ppermute | solution.py:15
  113.3 18.0 %collective-permute-start.10 = (bf16[2,128,1536]{2,1,0:T(8,128)(2,1)S(1)}, bf16[2,128,1536]{2,1,0:T(8,128)(2,1)S(1)}, u32[]{:S(2)}, u32[]{:S(2)}) collective-permute-start(bf16[2,128,1536]{2,1,0:T(8,128)(2,1)S(1)} %slice.44), channel_id=1, source_target_pairs={{0,24},{8,0},{16,8},{24,16},{1,25},{9,1},{17,9},{25,17},{2,26},{10... | collective-permute-start | bytes 2359304 | tf_op jit(solution)/shard_map/ppermute | solution.py:15
  117.1 17.0 %collective-permute-start.17 = (bf16[2,128,1536]{2,1,0:T(8,128)(2,1)S(1)}, bf16[2,128,1536]{2,1,0:T(8,128)(2,1)S(1)}, u32[]{:S(2)}, u32[]{:S(2)}) collective-permute-start(bf16[2,128,1536]{2,1,0:T(8,128)(2,1)S(1)} %slice.48), channel_id=1, source_target_pairs={{0,2},{2,4},{4,6},{6,0},{1,3},{3,5},{5,7},{7,1},{8,10},{10,12},{12... | collective-permute-start | bytes 2359304 | tf_op jit(solution)/shard_map/ppermute | solution.py:15
  117.6 16.6 %collective-permute-start.18 = (bf16[2,128,1536]{2,1,0:T(8,128)(2,1)S(1)}, bf16[2,128,1536]{2,1,0:T(8,128)(2,1)S(1)}, u32[]{:S(2)}, u32[]{:S(2)}) collective-permute-start(bf16[2,128,1536]{2,1,0:T(8,128)(2,1)S(1)} %slice.49), channel_id=1, source_target_pairs={{0,6},{2,0},{4,2},{6,4},{1,7},{3,1},{5,3},{7,5},{8,14},{10,8},{12,... | collective-permute-start | bytes 2359304 | tf_op jit(solution)/shard_map/ppermute | solution.py:15
  131.3 10.7 %copy-start = (bf16[4,4,128,1536]{3,2,0,1:T(8,128)(2,1)}, bf16[4,4,128,1536]{3,2,0,1:T(8,128)(2,1)S(1)}, u32[]{:S(2)}) copy-start(bf16[4,4,128,1536]{3,2,0,1:T(8,128)(2,1)S(1)} %bitcast_dynamic-update-slice_fusion.7) | copy-start | bytes 18874372
  134.2 7.8 %copy-start.1 = (bf16[4,4,128,1536]{3,2,0,1:T(8,128)(2,1)}, bf16[4,4,128,1536]{3,2,0,1:T(8,128)(2,1)S(1)}, u32[]{:S(2)}) copy-start(bf16[4,4,128,1536]{3,2,0,1:T(8,128)(2,1)S(1)} %bitcast_dynamic-update-slice_fusion.9) | copy-start | bytes 18874372
  134.3 7.8 %copy-start.2 = (bf16[1,256,4,1,256]{4,3,2,1,0:T(2,128)(2,1)S(1)}, bf16[1,256,4,1,256]{4,3,2,1,0:T(2,128)(2,1)}, u32[]{:S(2)}) copy-start(bf16[1,256,4,1,256]{4,3,2,1,0:T(2,128)(2,1)} %get-tuple-element.11) | copy-start | bytes 1572868
  142.1 35.1 %collective-permute-start.23 = (f32[256,1536]{1,0:T(8,128)}, f32[256,1536]{1,0:T(8,128)}, u32[]{:S(2)}, u32[]{:S(2)}) collective-permute-start(f32[256,1536]{1,0:T(8,128)} %fusion.4), channel_id=1, source_target_pairs={{0,1},{1,0},{2,3},{3,2},{4,5},{5,4},{6,7},{7,6},{8,9},{9,8},{10,11... | collective-permute-start | bytes 4718600 | tf_op jit(solution)/shard_map/ppermute | solution.py:15
  143.0 15.8 %collective-permute-start = (bf16[256,4,256]{2,0,1:T(8,128)(2,1)}, bf16[256,4,256]{2,0,1:T(8,128)(2,1)}, u32[]{:S(2)}, u32[]{:S(2)}) collective-permute-start(bf16[256,4,256]{2,0,1:T(8,128)(2,1)} %bitcast.129), channel_id=1, source_target_pairs={{0,32},{1,33},{32,64},{33,65},{64,96},{65,97},{96,0},{97,1},{2,34}... | collective-permute-start | bytes 1572872 | tf_op jit(solution)/shard_map/ppermute | solution.py:85
  146.2 28.3 %collective-permute-start.1 = (bf16[256,4,256]{2,0,1:T(8,128)(2,1)}, bf16[256,4,256]{2,0,1:T(8,128)(2,1)}, u32[]{:S(2)}, u32[]{:S(2)}) collective-permute-start(bf16[256,4,256]{2,0,1:T(8,128)(2,1)} %bitcast.128), channel_id=1, source_target_pairs={{0,64},{1,65},{32,96},{33,97},{64,0},{65,1},{96,32},{97,33},{2,66}... | collective-permute-start | bytes 1572872 | tf_op jit(solution)/shard_map/ppermute | solution.py:85
  151.5 5.2 %copy-start.6 = (f32[1,1536]{1,0:T(1,128)S(1)}, f32[1,1536]{1,0:T(1,128)}, u32[]{:S(2)}) copy-start(f32[1,1536]{1,0:T(1,128)} %param.8) | copy-start | bytes 18436
  151.5 24.9 %collective-permute-start.2 = (bf16[256,4,256]{2,0,1:T(8,128)(2,1)S(1)}, bf16[256,4,256]{2,0,1:T(8,128)(2,1)S(1)}, u32[]{:S(2)}, u32[]{:S(2)}) collective-permute-start(bf16[256,4,256]{2,0,1:T(8,128)(2,1)S(1)} %bitcast.136), channel_id=1, source_target_pairs={{0,96},{1,97},{32,0},{33,1},{64,32},{65,33},{96,64},{97,65},{2,98}... | collective-permute-start | bytes 1572872 | tf_op jit(solution)/shard_map/ppermute | solution.py:85
  155.7 21.5 %copy-start.5 = (bf16[32,8,4,384]{3,1,2,0:T(8,128)(2,1)S(1)}, bf16[32,8,4,384]{3,1,2,0:T(8,128)(2,1)}, u32[]{:S(2)}) copy-start(bf16[32,8,4,384]{3,1,2,0:T(8,128)(2,1)} %copy-done.4) | copy-start | bytes 2359300
  155.7 21.5 %copy-start.7 = (f32[1,256]{1,0:T(1,128)S(1)}, f32[1,256]{1,0:T(1,128)}, u32[]{:S(2)}) copy-start(f32[1,256]{1,0:T(1,128)} %param.7) | copy-start | bytes 3076
  (2 other events, 10.0 us)
